TPU v7x, 32 devices: a whole 2x2x4 slice. The times are simulated.
32 devices in a mesh: dp: 16 (over z, x, core), tensor: 2 (over y).
Axes of the slice: x: 2, y: 2, z: 4, core: 2. Of those that a mesh axis runs over, the one named last changes fastest.
Arguments:
- tokens: bfloat16 [16384, 1024], P('dp'), may hold values from -6 to 6
- cotangent: bfloat16 [16384, 1024], P('dp'), may hold values from -6 to 6
- lengths: int32 [16, 8], P('dp'), may hold values from 0 to 1024, as said below
- norm_gain: float32 [1024], replicated, may hold values from 0.5 to 1.5
- query_weight: bfloat16 [1024, 512], P(None, 'tensor'), may hold values from -0.1875 to 0.1875
- key_weight: bfloat16 [1024, 128], P(None, 'tensor'), may hold values from -0.1875 to 0.1875
- value_weight: bfloat16 [1024, 128], P(None, 'tensor'), may hold values from -0.1875 to 0.1875
- attn_out_weight: bfloat16 [512, 1024], P('tensor'), may hold values from -4 to 4
- z_weight: bfloat16 [1024, 1536], P(None, 'tensor'), may hold values from -0.1875 to 0.1875
- x_weight: bfloat16 [1024, 1536], P(None, 'tensor'), may hold values from -0.1875 to 0.1875
- bc_weight: bfloat16 [1024, 256], replicated, may hold values from -0.1875 to 0.1875
- dt_weight: bfloat16 [1024, 24], P(None, 'tensor'), may hold values from -0.09375 to 0.09375
- conv_x: bfloat16 [4, 1536], P(None, 'tensor'), may hold values from -3 to 3
- conv_x_bias: bfloat16 [1536], P('tensor'), may hold values from -3 to 3
- conv_bc: bfloat16 [4, 256], replicated, may hold values from -3 to 3
- conv_bc_bias: bfloat16 [256], replicated, may hold values from -3 to 3
- dt_bias: float32 [24], P('tensor'), may hold values from -6 to -2
- a_log: float32 [24], P('tensor'), may hold values from 0 to 2.7
- skip_gain: float32 [24], P('tensor'), may hold values from 0.5 to 2
- mixer_gain: float32 [1536], P('tensor'), may hold values from 0.5 to 1.5
- mamba_out_weight: bfloat16 [1536, 1024], P('tensor'), may hold values from -0.15625 to 0.15625
- ffn_gain: float32 [1024], replicated, may hold values from 0.5 to 1.5
- gate_weight: bfloat16 [1024, 2048], P(None, 'tensor'), may hold values from -0.1875 to 0.1875
- up_weight: bfloat16 [1024, 2048], P(None, 'tensor'), may hold values from -0.1875 to 0.1875
- down_weight: bfloat16 [2048, 1024], P('tensor'), may hold values from -0.125 to 0.125
Outputs:
- block_output: bfloat16 [16384, 1024], P('dp')
- tokens_grad: bfloat16 [16384, 1024], P('dp')
- norm_gain_grad: float32 [1024], replicated
- query_weight_grad: float32 [1024, 512], P('dp', 'tensor')
- key_weight_grad: float32 [1024, 128], P('dp', 'tensor')
- value_weight_grad: float32 [1024, 128], P('dp', 'tensor')
- attn_out_weight_grad: float32 [512, 1024], P('tensor', 'dp')
- z_weight_grad: float32 [1024, 1536], P('dp', 'tensor')
- x_weight_grad: float32 [1024, 1536], P('dp', 'tensor')
- bc_weight_grad: float32 [1024, 256], P('dp')
- dt_weight_grad: float32 [1024, 24], P('dp', 'tensor')
- conv_x_grad: float32 [4, 1536], P(None, 'tensor')
- conv_x_bias_grad: float32 [1536], P('tensor')
- conv_bc_grad: float32 [4, 256], replicated
- conv_bc_bias_grad: float32 [256], replicated
- dt_bias_grad: float32 [24], P('tensor')
- a_log_grad: float32 [24], P('tensor')
- skip_gain_grad: float32 [24], P('tensor')
- mixer_gain_grad: float32 [1536], P('tensor')
- mamba_out_weight_grad: float32 [1536, 1024], P('tensor', 'dp')
- ffn_gain_grad: float32 [1024], replicated
- gate_weight_grad: float32 [1024, 2048], P('dp', 'tensor')
- up_weight_grad: float32 [1024, 2048], P('dp', 'tensor')
- down_weight_grad: float32 [2048, 1024], P('tensor', 'dp')
Inputs may be any that keep to these rules, and one draw needn't show every extreme that they name: In each row the nonzero lengths come first; ceil(length / 128) summed over a row is at most 8; some entry equals 1024.
All inputs are finite; a program needn't handle non-finite values.
Results may differ from a plain program's by a relative error of at most 0.015.
Values sent between devices are 32-bit elements; how exact they have to be, the bound alone decides.
No kernel may reach another device: no remote copies, remote signals or barrier semaphores. Data moves between devices by JAX's collectives and lax.ppermute only.
A program may use at most 192 MiB of HBM per device.

v0:
```python
from functools import partial

import jax
import jax.numpy as jnp
from jax import lax
from jax.sharding import PartitionSpec as P

SSM_HEADS = 24
SSM_HEAD_DIM = 64
STATE = 128
CONV_WIDTH = 4
HEAD_DIM = 64
BLOCK = 128


EPSILON = 1e-05
ROPE_BASE = 100000000000.0
MASKED = -1e30
PRECISE = lax.Precision.HIGHEST


def layout(lengths_row):
    row_count = lengths_row.shape[0] * BLOCK
    block_use = (lengths_row + BLOCK - 1) // BLOCK
    starts = (jnp.cumsum(block_use) - block_use) * BLOCK
    finish = starts + block_use * BLOCK
    slot_ids = jnp.arange(row_count, dtype=jnp.int32)
    inside = (
        (slot_ids[:, None] >= starts[None, :]) & (slot_ids[:, None] < finish[None, :])
    ).astype(jnp.int32)
    seq_start = jnp.sum(inside * starts[None, :], axis=1)
    seq_length = jnp.sum(inside * lengths_row[None, :], axis=1)
    labels = jnp.arange(1, lengths_row.shape[0] + 1, dtype=jnp.int32)
    owners = jnp.sum(inside * labels[None, :], axis=1)
    position = slot_ids - seq_start
    validity = (position < seq_length).astype(jnp.float32)
    carry_on = (position[::BLOCK] != 0).astype(jnp.float32)
    return (position, owners, validity, carry_on)


def project(left, right):
    return jnp.dot(left, right, preferred_element_type=jnp.float32)


def outer_rows(left, right):
    return lax.dot_general(
        left, right, (((0,), (0,)), ((), ())), preferred_element_type=jnp.float32
    )


def back_project(grad_rows, weight):
    return lax.dot_general(
        grad_rows, weight, (((1,), (1,)), ((), ())), preferred_element_type=jnp.float32
    )


def rms_norm(values, gain_vector):
    scaling = lax.rsqrt(jnp.mean(values * values, axis=-1, keepdims=True) + EPSILON)
    return values * scaling * gain_vector


def swiglu(gate_values, up_values):
    return jax.nn.silu(gate_values) * up_values


def rotate(values, position):
    halfway = HEAD_DIM // 2
    frequency = ROPE_BASE ** (-2.0 * jnp.arange(halfway, dtype=jnp.float32) / HEAD_DIM)
    angles = position.astype(jnp.float32)[:, None] * frequency[None, :]
    target_shape = (values.shape[0],) + (1,) * (values.ndim - 2) + (halfway,)
    cosine = jnp.cos(angles).reshape(target_shape)
    sine_part = jnp.sin(angles).reshape(target_shape)
    leading = values[..., :halfway]
    second = values[..., halfway:]
    return jnp.concatenate(
        [leading * cosine - second * sine_part, second * cosine + leading * sine_part], axis=-1
    )


def convolve(values, kernel, offset_terms, position):
    summed = offset_terms[None, :] + kernel[0][None, :] * values
    for shift_by in range(1, CONV_WIDTH):
        earlier = jnp.concatenate(
            [jnp.zeros((shift_by, values.shape[1]), values.dtype), values[:-shift_by]], axis=0
        )
        reached = (position >= shift_by).astype(values.dtype)
        summed = summed + kernel[shift_by][None, :] * earlier * reached[:, None]
    return jax.nn.silu(summed)


def mamba_core(inputs, bc_values, gate_lin, step_lin, step_bias, log_rates, skip_terms, carry_on):
    row_count, head_count = step_lin.shape
    blocks_in = row_count // BLOCK
    step_size = jax.nn.softplus(step_lin + step_bias[None, :])
    decay_rate = -jnp.exp(log_rates)
    streams = inputs.reshape(blocks_in, BLOCK, head_count, SSM_HEAD_DIM)
    write_keys = bc_values[:, :STATE].reshape(blocks_in, BLOCK, STATE)
    read_keys = bc_values[:, STATE:].reshape(blocks_in, BLOCK, STATE)
    steps_in = step_size.reshape(blocks_in, BLOCK, head_count)
    log_decay = jnp.cumsum(steps_in * decay_rate[None, None, :], axis=1)
    causal = jnp.arange(BLOCK)[:, None] >= jnp.arange(BLOCK)[None, :]
    gap_matrix = log_decay[:, :, None, :] - log_decay[:, None, :, :]
    mixing = jnp.exp(jnp.where(causal[None, :, :, None], gap_matrix, MASKED))
    intersection = jnp.einsum("ctn,csn->cts", read_keys, write_keys, precision=PRECISE)
    scaled = streams * steps_in[..., None]
    within = jnp.einsum(
        "ctsh,cshp->cthp", intersection[..., None] * mixing, scaled, precision=PRECISE
    )
    to_end = jnp.exp(log_decay[:, -1:, :] - log_decay)
    pieces = jnp.einsum("csn,cshp->chnp", write_keys, scaled * to_end[..., None], precision=PRECISE)
    decays = jnp.exp(log_decay[:, -1, :])

    def advance(carried, items):
        piece_now, decay_now, keep_now = items
        entering = carried * keep_now
        return (decay_now[:, None, None] * entering + piece_now, entering)

    start_state = jnp.zeros((head_count, STATE, SSM_HEAD_DIM), jnp.float32)
    final_state, entering = lax.scan(advance, start_state, (pieces, decays, carry_on))
    across = (
        jnp.einsum("ctn,chnp->cthp", read_keys, entering, precision=PRECISE)
        * jnp.exp(log_decay)[..., None]
    )
    result = within + across + skip_terms[None, None, :, None] * streams
    gated = result * jax.nn.silu(gate_lin.reshape(blocks_in, BLOCK, head_count, SSM_HEAD_DIM))
    return gated.reshape(row_count, head_count * SSM_HEAD_DIM)


def block_scores(query_part, key_rows, owners, offset, slot_ids):
    block_rows = query_part.shape[0]
    scores = jnp.einsum(
        "shgd,thd->hgst", query_part, key_rows, preferred_element_type=jnp.float32
    ) * HEAD_DIM ** (-0.5)
    query_ids = offset + jnp.arange(block_rows, dtype=jnp.int32)
    query_owner = lax.dynamic_slice_in_dim(owners, offset, block_rows, 0)
    allowed = (query_owner[:, None] == owners[None, :]) & (slot_ids[None, :] <= query_ids[:, None])
    return jnp.where(allowed, scores, MASKED)


def attend_forward(queries, key_rows, value_rows, owners):
    row_count = queries.shape[0]
    block_rows = min(512, row_count)
    slot_ids = jnp.arange(row_count, dtype=jnp.int32)

    def one_block(offset):
        query_part = lax.dynamic_slice_in_dim(queries, offset, block_rows, 0)
        scores = block_scores(query_part, key_rows, owners, offset, slot_ids)
        maxima = jnp.max(scores, axis=-1, keepdims=True)
        expo = jnp.exp(scores - maxima)
        totals = jnp.sum(expo, axis=-1, keepdims=True)
        probabilities = (expo / totals).astype(jnp.bfloat16)
        result = jnp.einsum(
            "hgst,thd->shgd", probabilities, value_rows, preferred_element_type=jnp.float32
        )
        return (result, (maxima + jnp.log(totals))[..., 0])

    offsets = jnp.arange(0, row_count, block_rows, dtype=jnp.int32)
    results, log_totals = lax.map(one_block, offsets)
    return (results.reshape(queries.shape), log_totals)


def attend_backward(queries, key_rows, value_rows, owners, log_totals, grad_out):
    row_count = queries.shape[0]
    block_rows = min(512, row_count)
    slot_ids = jnp.arange(row_count, dtype=jnp.int32)
    score_scale = HEAD_DIM ** (-0.5)

    def one_block(carried, items):
        key_grad, value_grad = carried
        offset, totals = items
        query_part = lax.dynamic_slice_in_dim(queries, offset, block_rows, 0)
        grad_part = lax.dynamic_slice_in_dim(grad_out, offset, block_rows, 0)
        scores = block_scores(query_part, key_rows, owners, offset, slot_ids)
        probabilities = jnp.exp(scores - totals[..., None])
        value_grad = value_grad + jnp.einsum(
            "hgst,shgd->thd",
            probabilities.astype(jnp.bfloat16),
            grad_part,
            preferred_element_type=jnp.float32,
        )
        prob_grad = jnp.einsum(
            "shgd,thd->hgst", grad_part, value_rows, preferred_element_type=jnp.float32
        )
        score_grad_low = (
            probabilities * (prob_grad - jnp.sum(probabilities * prob_grad, axis=-1, keepdims=True))
        ).astype(jnp.bfloat16)
        query_grad = (
            jnp.einsum(
                "hgst,thd->shgd", score_grad_low, key_rows, preferred_element_type=jnp.float32
            )
            * score_scale
        )
        key_grad = (
            key_grad
            + jnp.einsum(
                "hgst,shgd->thd", score_grad_low, query_part, preferred_element_type=jnp.float32
            )
            * score_scale
        )
        return ((key_grad, value_grad), query_grad)

    offsets = jnp.arange(0, row_count, block_rows, dtype=jnp.int32)
    zeros_kv = jnp.zeros(key_rows.shape, jnp.float32)
    (key_grad, value_grad), query_grads = lax.scan(
        one_block, (zeros_kv, zeros_kv), (offsets, log_totals)
    )
    return (query_grads.reshape(queries.shape), key_grad, value_grad)


def body(
    tokens,
    cotangent,
    lengths,
    norm_gain,
    query_weight,
    key_weight,
    value_weight,
    attn_out_weight,
    z_weight,
    x_weight,
    bc_weight,
    dt_weight,
    conv_x,
    conv_x_bias,
    conv_bc,
    conv_bc_bias,
    dt_bias,
    a_log,
    skip_gain,
    mixer_gain,
    mamba_out_weight,
    ffn_gain,
    gate_weight,
    up_weight,
    down_weight,
):
    position, owners, validity, carry_on = layout(lengths[0])
    row_count = tokens.shape[0]
    kv_local = key_weight.shape[1] // HEAD_DIM
    grouping = query_weight.shape[1] // key_weight.shape[1]
    group_width = SSM_HEADS * SSM_HEAD_DIM
    valid_col = validity[:, None]
    tokens_wide = tokens.astype(jnp.float32)
    normed, first_norm_back = jax.vjp(rms_norm, tokens_wide, norm_gain)
    first_in = normed.astype(jnp.bfloat16)
    rotation = partial(rotate, position=position)
    query_lin = project(first_in, query_weight).reshape(row_count, kv_local, grouping, HEAD_DIM)
    key_lin = project(first_in, key_weight).reshape(row_count, kv_local, HEAD_DIM)
    value_rows = (
        project(first_in, value_weight).reshape(row_count, kv_local, HEAD_DIM).astype(jnp.bfloat16)
    )
    query_turned, query_unturn = jax.vjp(rotation, query_lin)
    key_turned, key_unturn = jax.vjp(rotation, key_lin)
    queries = query_turned.astype(jnp.bfloat16)
    key_rows = key_turned.astype(jnp.bfloat16)
    attended_wide, log_totals = attend_forward(queries, key_rows, value_rows, owners)
    attended = attended_wide.reshape(row_count, -1).astype(jnp.bfloat16)
    gate_lin = project(first_in, z_weight)
    stream_lin = project(first_in, x_weight)
    bc_lin = project(first_in, bc_weight)
    step_lin = project(first_in, dt_weight)
    causal_filter = partial(convolve, position=position)
    streams_wide, stream_back = jax.vjp(
        causal_filter, stream_lin, conv_x.astype(jnp.float32), conv_x_bias.astype(jnp.float32)
    )
    bc_wide, bc_back = jax.vjp(
        causal_filter, bc_lin, conv_bc.astype(jnp.float32), conv_bc_bias.astype(jnp.float32)
    )
    streams = streams_wide.astype(jnp.bfloat16)
    bc_values = bc_wide.astype(jnp.bfloat16)
    ssm_core = partial(mamba_core, carry_on=carry_on)
    gated_wide, core_back = jax.vjp(
        ssm_core,
        streams.astype(jnp.float32),
        bc_values.astype(jnp.float32),
        gate_lin,
        step_lin,
        dt_bias,
        a_log,
        skip_gain,
    )
    square_sum = lax.psum(jnp.sum(gated_wide * gated_wide, axis=-1), "tensor")
    group_scale = lax.rsqrt(square_sum / group_width + EPSILON)[:, None]
    normed_gated = gated_wide * group_scale
    mixed = (normed_gated * mixer_gain[None, :]).astype(jnp.bfloat16)
    branch_part = project(attended, attn_out_weight) + project(mixed, mamba_out_weight)
    branch = lax.psum(branch_part, "tensor")
    middle = tokens_wide + valid_col * branch
    second_wide, second_norm_back = jax.vjp(rms_norm, middle, ffn_gain)
    second_in = second_wide.astype(jnp.bfloat16)
    gate_values = project(second_in, gate_weight)
    up_values = project(second_in, up_weight)
    hidden_wide, hidden_back = jax.vjp(swiglu, gate_values, up_values)
    hidden = hidden_wide.astype(jnp.bfloat16)
    ffn_full = lax.psum(project(hidden, down_weight), "tensor")
    block_output = (middle + valid_col * ffn_full).astype(jnp.bfloat16)
    cot_wide = cotangent.astype(jnp.float32)
    grad_ffn = (valid_col * cot_wide).astype(jnp.bfloat16)
    down_grad = outer_rows(hidden, grad_ffn)
    grad_hidden = back_project(grad_ffn, down_weight)
    grad_gate_wide, grad_up_wide = hidden_back(grad_hidden)
    grad_gate = grad_gate_wide.astype(jnp.bfloat16)
    grad_up = grad_up_wide.astype(jnp.bfloat16)
    gate_grad = outer_rows(second_in, grad_gate)
    up_grad = outer_rows(second_in, grad_up)
    grad_second = lax.psum(
        back_project(grad_gate, gate_weight) + back_project(grad_up, up_weight), "tensor"
    )
    grad_middle_norm, ffn_gain_grad = second_norm_back(grad_second)
    grad_middle = cot_wide + grad_middle_norm
    grad_branch = (valid_col * grad_middle).astype(jnp.bfloat16)
    attn_out_grad = outer_rows(attended, grad_branch)
    mamba_out_grad = outer_rows(mixed, grad_branch)
    grad_attended = (
        back_project(grad_branch, attn_out_weight)
        .astype(jnp.bfloat16)
        .reshape(row_count, kv_local, grouping, HEAD_DIM)
    )
    grad_mixed = back_project(grad_branch, mamba_out_weight)
    gain_scaled = grad_mixed * mixer_gain[None, :]
    mixer_gain_grad = jnp.sum(grad_mixed * normed_gated, axis=0)
    cross_sum = lax.psum(jnp.sum(gain_scaled * normed_gated, axis=-1), "tensor")
    grad_gated = group_scale * (gain_scaled - normed_gated * (cross_sum / group_width)[:, None])
    grad_streams, grad_bc, grad_gate_lin, grad_step_lin, dt_bias_grad, a_log_grad, skip_grad = (
        core_back(grad_gated)
    )
    grad_stream_lin, conv_x_grad, conv_x_bias_grad = stream_back(grad_streams)
    grad_bc_lin, conv_bc_part, conv_bc_bias_part = bc_back(grad_bc)
    grad_query, grad_key, grad_value = attend_backward(
        queries, key_rows, value_rows, owners, log_totals, grad_attended
    )
    (grad_query_lin,) = query_unturn(grad_query)
    (grad_key_lin,) = key_unturn(grad_key)
    grad_query_low = grad_query_lin.reshape(row_count, -1).astype(jnp.bfloat16)
    grad_key_low = grad_key_lin.reshape(row_count, -1).astype(jnp.bfloat16)
    grad_value_low = grad_value.reshape(row_count, -1).astype(jnp.bfloat16)
    grad_gate_low = grad_gate_lin.astype(jnp.bfloat16)
    grad_stream_low = grad_stream_lin.astype(jnp.bfloat16)
    grad_step_low = grad_step_lin.astype(jnp.bfloat16)
    query_grad = outer_rows(first_in, grad_query_low)
    key_grad = outer_rows(first_in, grad_key_low)
    value_grad = outer_rows(first_in, grad_value_low)
    z_grad = outer_rows(first_in, grad_gate_low)
    x_grad = outer_rows(first_in, grad_stream_low)
    dt_grad = outer_rows(first_in, grad_step_low)
    bc_part = lax.dot_general(
        first_in.astype(jnp.float32), grad_bc_lin, (((0,), (0,)), ((), ())), precision=PRECISE
    )
    grad_first_part = (
        back_project(grad_query_low, query_weight)
        + back_project(grad_key_low, key_weight)
        + back_project(grad_value_low, value_weight)
        + back_project(grad_gate_low, z_weight)
        + back_project(grad_stream_low, x_weight)
        + back_project(grad_step_low, dt_weight)
        + lax.dot_general(
            grad_bc_lin, bc_weight.astype(jnp.float32), (((1,), (1,)), ((), ())), precision=PRECISE
        )
    )
    grad_first, bc_grad_full, conv_bc_grad, conv_bc_bias_grad = lax.psum(
        (grad_first_part, bc_part, conv_bc_part, conv_bc_bias_part), "tensor"
    )
    grad_tokens_norm, norm_gain_grad = first_norm_back(grad_first)
    tokens_grad = (grad_middle + grad_tokens_norm).astype(jnp.bfloat16)
    matrix_sums = (
        lax.psum_scatter(query_grad, "dp", scatter_dimension=0, tiled=True),
        lax.psum_scatter(key_grad, "dp", scatter_dimension=0, tiled=True),
        lax.psum_scatter(value_grad, "dp", scatter_dimension=0, tiled=True),
        lax.psum_scatter(attn_out_grad, "dp", scatter_dimension=1, tiled=True),
        lax.psum_scatter(z_grad, "dp", scatter_dimension=0, tiled=True),
        lax.psum_scatter(x_grad, "dp", scatter_dimension=0, tiled=True),
        lax.psum_scatter(bc_grad_full, "dp", scatter_dimension=0, tiled=True),
        lax.psum_scatter(dt_grad, "dp", scatter_dimension=0, tiled=True),
        lax.psum_scatter(mamba_out_grad, "dp", scatter_dimension=1, tiled=True),
        lax.psum_scatter(gate_grad, "dp", scatter_dimension=0, tiled=True),
        lax.psum_scatter(up_grad, "dp", scatter_dimension=0, tiled=True),
        lax.psum_scatter(down_grad, "dp", scatter_dimension=1, tiled=True),
    )
    vector_sums = lax.psum(
        (
            norm_gain_grad,
            conv_x_grad,
            conv_x_bias_grad,
            conv_bc_grad,
            conv_bc_bias_grad,
            dt_bias_grad,
            a_log_grad,
            skip_grad,
            mixer_gain_grad,
            ffn_gain_grad,
        ),
        "dp",
    )
    return (
        block_output,
        tokens_grad,
        vector_sums[0],
        matrix_sums[0],
        matrix_sums[1],
        matrix_sums[2],
        matrix_sums[3],
        matrix_sums[4],
        matrix_sums[5],
        matrix_sums[6],
        matrix_sums[7],
        vector_sums[1],
        vector_sums[2],
        vector_sums[3],
        vector_sums[4],
        vector_sums[5],
        vector_sums[6],
        vector_sums[7],
        vector_sums[8],
        matrix_sums[8],
        vector_sums[9],
        matrix_sums[9],
        matrix_sums[10],
        matrix_sums[11],
    )


def solution(mesh):
    return jax.shard_map(
        body,
        mesh=mesh,
        in_specs=(
            P("dp", None),
            P("dp", None),
            P("dp", None),
            P(),
            P(None, "tensor"),
            P(None, "tensor"),
            P(None, "tensor"),
            P("tensor", None),
            P(None, "tensor"),
            P(None, "tensor"),
            P(),
            P(None, "tensor"),
            P(None, "tensor"),
            P("tensor"),
            P(),
            P(),
            P("tensor"),
            P("tensor"),
            P("tensor"),
            P("tensor"),
            P("tensor", None),
            P(),
            P(None, "tensor"),
            P(None, "tensor"),
            P("tensor", None),
        ),
        out_specs=(
            P("dp", None),
            P("dp", None),
            P(),
            P("dp", "tensor"),
            P("dp", "tensor"),
            P("dp", "tensor"),
            P("tensor", "dp"),
            P("dp", "tensor"),
            P("dp", "tensor"),
            P("dp", None),
            P("dp", "tensor"),
            P(None, "tensor"),
            P("tensor"),
            P(),
            P(),
            P("tensor"),
            P("tensor"),
            P("tensor"),
            P("tensor"),
            P("tensor", "dp"),
            P(),
            P("dp", "tensor"),
            P("dp", "tensor"),
            P("tensor", "dp"),
        ),
        check_vma=False,
    )
```

profile of v0, /device:TPU:0, one launch (start us, length us, event | category | flops | bytes accessed | tf_op | source)
XLA Modules:
  0.0 1742.9 jit_solution(12957189305417658737)
XLA Ops:
  58.9 65.5 %while.63 = (s32[]{:T(128)}, f32[12,128,64]{2,1,0:T(8,128)S(1)}, f32[8,12,128,64]{3,2,1,0:T(8,128)}, f32[8,12,1,1]{1,3,2,0:T(1,128)}, f32[8,12]{1,0:T(8,128)}, /...) while((s32[]{:T(128)}, f32[12,128,64]{2,1,0:T(8,128)S(1)}, ...), condition=%wide.region_11.12_spmd.clone, body=%wide.region_10.11_spmd.clone.sunk | while | flops 589827 | bytes 3934992 | solution.py:119
  149.5 13.6 multiply_reduce_fusion.13
  182.9 25.7 %while.62 = (s32[]{:T(128)}, bf16[2,512,1,4,64]{1,4,3,2,0:T(8,128)(2,1)}, f32[2,1,4,512]{3,2,1,0:T(4,128)}, s32[2]{0:T(128)}, s32[1024]{0:T(1024)S(1)}, /*index=...) while((s32[]{:T(128)}, ...), condition=%wide.region_8.9_spmd.clone, body=%wide.region_5.8_spmd.clone.sunk | while | flops 563608064 | bytes 32717088 | solution.py:158
  217.8 109.8 %all-reduce.35.cloned.1.call-done = f32[1024,1024]{1,0:T(8,128)} async-done(((f32[1024,1024]{1,0:T(8,128)}), f32[1024,1024]{1,0:T(8,128)}) %all-reduce.35.cloned.1.call-update) | async-done | bytes 4194320 | tf_op jit(solution)/shard_map/psum | solution.py:287
  357.8 102.0 %all-reduce.37.cloned.1.call-done = f32[1024,1024]{1,0:T(8,128)} async-done(((f32[1024,1024]{1,0:T(8,128)}), f32[1024,1024]{1,0:T(8,128)}) %all-reduce.37.cloned.1.call-update) | async-done | bytes 4194320 | tf_op jit(solution)/shard_map/psum | solution.py:306
  501.9 11.0 fusion.149
  513.0 15.1 fusion.94
  534.9 45.4 %while.65 = (s32[]{:T(128)}, f32[12,128,64]{2,1,0:T(8,128)S(1)}, f32[8,12,128,64]{3,2,1,0:T(8,128)}, f32[8,12]{1,0:T(8,128)S(1)}, f32[8,12,128,64]{2,3,1,0:T(8,1...) while((s32[]{:T(128)}, f32[12,128,64]{2,1,0:T(8,128)S(1)}, ...), condition=%wide.region_26.27_spmd.clone, body=%wide.region_24.26_spmd.clone.sunk | while | flops 688120 | bytes 4325832 | solution.py:119
  580.3 15.1 fusion.152
  602.4 65.5 %while.64 = (s32[]{:T(128)}, f32[1024,1,64]{0,2,1:T(8,128)S(1)}, f32[1024,1,64]{0,2,1:T(8,128)}, f32[2,512,1,4,64]{1,0,4,3,2:T(2,128)}, s32[2]{0:T(128)S(1)}, /*...) while((s32[]{:T(128)}, f32[1024,1,64]{0,2,1:T(8,128)S(1)}, ...), condition=%wide.region_21.22_spmd.clone, body=%wide.region_19.21_spmd.clone.sunk | while | flops 1375664640 | bytes 122624344 | solution.py:204
  757.8 13.1 add_add_fusion.2
  770.9 25.8 %reduce-scatter.35.cloned.1.call-done = f32[64,256]{1,0:T(8,128)} async-done(((f32[1024,256]{1,0:T(8,128)}), f32[64,256]{1,0:T(8,128)}) %reduce-scatter.35.cloned.1.call-update) | async-done | bytes 65552 | tf_op jit(solution)/shard_map/reduce_scatter | solution.py:372
  857.0 199.7 %all-reduce.39.cloned.1.call-done = (f32[1024,1024]{1,0:T(8,128)}, f32[1024,1024]{1,0:T(8,128)}, f32[64,256]{1,0:T(8,128)}) async-done(((f32[1024,1024]{1,0:T(8,128)}, f32[1024,1024]{1,0:T(8,128)}, f32[64,256]{1,0:T(8,128)}), (f32[1024,1024]{1,0:T(8,128)}, f32[1024,1024]{1,0:T(8,128)}, f32[64,256]{1,0:T(8,128)})) %all-reduce.39.cloned.1.call-update) | async-done | bytes 8454160 | tf_op jit(solution)/shard_map/psum | solution.py:295
  1060.3 61.6 %all-reduce.28 = (f32[1024]{0:T(1024)}, f32[4,768]{1,0:T(4,128)}, f32[768]{0:T(1024)}, f32[4,256]{1,0:T(4,128)}, f32[256]{0:T(256)}, /*index=5*/f32[12]{0:T(128)...) all-reduce(f32[1024]{0:T(1024)S(1)} %get-tuple-element.518, ...), channel_id=1, replica_groups=mesh['dp'=16,'tensor'=2] {'dp'}, use_global_device_ids=true, to_apply=%region_38.39 | all-reduce | flops 7972 | bytes 63776 | tf_op jit(solution)/shard_map/psum | solution.py:379
  1122.0 10.7 fusion.89
  1132.7 43.6 %reduce-scatter.19.cloned.1.call-done = f32[64,64]{1,0:T(8,128)} async-done(((f32[1024,64]{1,0:T(8,128)}), f32[64,64]{1,0:T(8,128)}) %reduce-scatter.19.cloned.1.call-update) | async-done | bytes 16400 | tf_op jit(solution)/shard_map/reduce_scatter | solution.py:368
  1176.2 60.8 %reduce-scatter.15.cloned.1.call-done = f32[64,256]{1,0:T(8,128)} async-done(((f32[1024,256]{1,0:T(8,128)}), f32[64,256]{1,0:T(8,128)}) %reduce-scatter.15.cloned.1.call-update) | async-done | bytes 65552 | tf_op jit(solution)/shard_map/reduce_scatter | solution.py:366
  1237.0 60.8 %reduce-scatter.21.cloned.1.call-done = f32[256,64]{0,1:T(8,128)} async-done(((f32[256,1024]{0,1:T(8,128)}), f32[256,64]{0,1:T(8,128)}) %reduce-scatter.21.cloned.1.call-update) | async-done | bytes 65552 | tf_op jit(solution)/shard_map/reduce_scatter | solution.py:369
  1297.9 76.2 %reduce-scatter.29.cloned.1.call-done = f32[64,1024]{1,0:T(8,128)} async-done(((f32[1024,1024]{1,0:T(8,128)}), f32[64,1024]{1,0:T(8,128)}) %reduce-scatter.29.cloned.1.call-update) | async-done | bytes 262160 | tf_op jit(solution)/shard_map/reduce_scatter | solution.py:375
  1374.0 76.3 %reduce-scatter.31.cloned.1.call-done = f32[64,1024]{1,0:T(8,128)} async-done(((f32[1024,1024]{1,0:T(8,128)}), f32[64,1024]{1,0:T(8,128)}) %reduce-scatter.31.cloned.1.call-update) | async-done | bytes 262160 | tf_op jit(solution)/shard_map/reduce_scatter | solution.py:376
  1450.4 76.2 %reduce-scatter.33.cloned.1.call-done = f32[1024,64]{0,1:T(8,128)} async-done(((f32[1024,1024]{0,1:T(8,128)}), f32[1024,64]{0,1:T(8,128)}) %reduce-scatter.33.cloned.1.call-update) | async-done | bytes 262160 | tf_op jit(solution)/shard_map/reduce_scatter | solution.py:377
  1526.5 69.7 %reduce-scatter.27.cloned.1.call-done = f32[768,64]{0,1:T(8,128)} async-done(((f32[768,1024]{0,1:T(8,128)}), f32[768,64]{0,1:T(8,128)}) %reduce-scatter.27.cloned.1.call-update) | async-done | bytes 196624 | tf_op jit(solution)/shard_map/reduce_scatter | solution.py:374
  1596.3 69.6 %reduce-scatter.25.cloned.1.call-done = f32[64,768]{1,0:T(8,128)} async-done(((f32[1024,768]{1,0:T(8,128)}), f32[64,768]{1,0:T(8,128)}) %reduce-scatter.25.cloned.1.call-update) | async-done | bytes 196624 | tf_op jit(solution)/shard_map/reduce_scatter | solution.py:371
  1665.8 69.7 %reduce-scatter.23.cloned.1.call-done = f32[64,768]{1,0:T(8,128)} async-done(((f32[1024,768]{1,0:T(8,128)}), f32[64,768]{1,0:T(8,128)}) %reduce-scatter.23.cloned.1.call-update) | async-done | bytes 196624 | tf_op jit(solution)/shard_map/reduce_scatter | solution.py:370
  (729 shorter events, 536.8 us)
Async XLA Ops:
  7.2 331.9 %copy-start = (bf16[1024,1024]{1,0:T(8,128)(2,1)S(1)}, bf16[1024,1024]{1,0:T(8,128)(2,1)}, u32[]{:S(2)}) copy-start(bf16[1024,1024]{1,0:T(8,128)(2,1)} %param.57) | copy-start | bytes 6291460
  7.2 320.4 %all-reduce.35.cloned.1.call-start = ((), (), s32[]{:S(2)}) async-start(), calls=%async_computation.12 | async-start | bytes 8388608 | tf_op jit(solution)/shard_map/psum | solution.py:287
  14.3 134.2 %copy-start.67 = (f32[8,128,12]{1,2,0:T(8,128)}, f32[8,128,12]{1,2,0:T(8,128)S(1)}, u32[]{:S(2)}) copy-start(f32[8,128,12]{1,2,0:T(8,128)S(1)} %copy.143) | copy-start | bytes 147460
  24.4 156.9 %copy-start.101 = (f32[1024]{0:T(1024)}, f32[1024]{0:T(1024)S(1)}, u32[]{:S(2)}) copy-start(f32[1024]{0:T(1024)S(1)} %get-tuple-element.682) | copy-start | bytes 12292
  24.4 440.6 %copy-start.111 = (f32[1024]{0:T(1024)}, f32[1024]{0:T(1024)S(1)}, u32[]{:S(2)}) copy-start(f32[1024]{0:T(1024)S(1)} %get-tuple-element.678) | copy-start | bytes 12292
  217.7 242.1 %all-reduce.37.cloned.1.call-start = ((), (), s32[]{:S(2)}) async-start(), calls=%async_computation.13 | async-start | bytes 8388608 | tf_op jit(solution)/shard_map/psum | solution.py:306
  351.7 445.1 %reduce-scatter.35.cloned.1.call-start = ((), (), s32[]{:S(2)}) async-start(), calls=%async_computation.24 | async-start | bytes 1114112 | tf_op jit(solution)/shard_map/reduce_scatter | solution.py:372
  739.0 116.5 %reduce-scatter.37.cloned.1.call-start = ((), (), s32[]{:S(2)}) async-start(), calls=%async_computation.25 | async-start | bytes 557056
  757.8 298.9 %all-reduce.39.cloned.1.call-start = ((), (), s32[]{:S(2)}) async-start(), calls=%async_computation.26 | async-start | bytes 16908288 | tf_op jit(solution)/shard_map/psum | solution.py:295
  796.8 335.8 %reduce-scatter.17.cloned.1.call-start = ((), (), s32[]{:S(2)}) async-start(), calls=%async_computation.15 | async-start | bytes 557056 | tf_op jit(solution)/shard_map/reduce_scatter | solution.py:367
  798.4 377.8 %reduce-scatter.19.cloned.1.call-start = ((), (), s32[]{:S(2)}) async-start(), calls=%async_computation.16 | async-start | bytes 557056 | tf_op jit(solution)/shard_map/reduce_scatter | solution.py:368
  800.1 436.9 %reduce-scatter.15.cloned.1.call-start = ((), (), s32[]{:S(2)}) async-start(), calls=%async_computation.14 | async-start | bytes 1114112 | tf_op jit(solution)/shard_map/reduce_scatter | solution.py:366
  801.9 496.0 %reduce-scatter.21.cloned.1.call-start = ((), (), s32[]{:S(2)}) async-start(), calls=%async_computation.17 | async-start | bytes 1114112 | tf_op jit(solution)/shard_map/reduce_scatter | solution.py:369
  805.5 568.5 %reduce-scatter.29.cloned.1.call-start = ((), (), s32[]{:S(2)}) async-start(), calls=%async_computation.21 | async-start | bytes 4456448 | tf_op jit(solution)/shard_map/reduce_scatter | solution.py:375
  812.3 638.1 %reduce-scatter.31.cloned.1.call-start = ((), (), s32[]{:S(2)}) async-start(), calls=%async_computation.22 | async-start | bytes 4456448 | tf_op jit(solution)/shard_map/reduce_scatter | solution.py:376
  819.0 707.5 %reduce-scatter.33.cloned.1.call-start = ((), (), s32[]{:S(2)}) async-start(), calls=%async_computation.23 | async-start | bytes 4456448 | tf_op jit(solution)/shard_map/reduce_scatter | solution.py:377
  826.3 770.0 %reduce-scatter.27.cloned.1.call-start = ((), (), s32[]{:S(2)}) async-start(), calls=%async_computation.20 | async-start | bytes 3342336 | tf_op jit(solution)/shard_map/reduce_scatter | solution.py:374
  833.2 832.7 %reduce-scatter.25.cloned.1.call-start = ((), (), s32[]{:S(2)}) async-start(), calls=%async_computation.19 | async-start | bytes 3342336 | tf_op jit(solution)/shard_map/reduce_scatter | solution.py:371
  838.3 897.2 %reduce-scatter.23.cloned.1.call-start = ((), (), s32[]{:S(2)}) async-start(), calls=%async_computation.18 | async-start | bytes 3342336 | tf_op jit(solution)/shard_map/reduce_scatter | solution.py:370
  843.5 213.1 %copy-start.15 = (bf16[1024,1024]{1,0:T(8,128)(2,1)S(1)}, bf16[1024,1024]{1,0:T(8,128)(2,1)}, u32[]{:S(2)}) copy-start(bf16[1024,1024]{1,0:T(8,128)(2,1)} %param.33) | copy-start | bytes 6291460
  843.6 213.1 %copy-start.114 = (f32[1024]{0:T(1024)S(1)}, f32[1024]{0:T(1024)}, u32[]{:S(2)}) copy-start(f32[1024]{0:T(1024)} %copy-done.113) | copy-start | bytes 12292
  843.6 213.1 %copy-start.129 = (f32[1024]{0:T(1024)S(1)}, f32[1024]{0:T(1024)}, u32[]{:S(2)}) copy-start(f32[1024]{0:T(1024)} %param.36) | copy-start | bytes 12292
  1122.0 613.5 %copy-start.108 = (f32[64,256]{1,0:T(8,128)S(1)}, f32[64,256]{1,0:T(8,128)}, u32[]{:S(2)}) copy-start(f32[64,256]{1,0:T(8,128)} %get-tuple-element.1061) | copy-start | bytes 196612
  1122.0 614.2 %copy-start.1 = (bf16[1024,1024]{1,0:T(8,128)(2,1)S(1)}, bf16[1024,1024]{1,0:T(8,128)(2,1)}, u32[]{:S(2)}) copy-start(bf16[1024,1024]{1,0:T(8,128)(2,1)} %param.57) | copy-start | bytes 6291460
  (179 other events, 1608.8 us)
Sparse Core Ops, SparseCore 0:
  217.8 109.6 all-reduce.34
  351.8 107.9 all-reduce.36
  739.2 57.5 reduce-scatter.34
  800.2 55.3 reduce-scatter.36
  858.1 198.4 all-reduce.38
  1060.6 56.1 reduce-scatter.16
  1121.0 55.1 reduce-scatter.18
  1180.4 56.5 reduce-scatter.14
  1241.2 56.5 reduce-scatter.20
  1302.1 71.8 reduce-scatter.28
  1378.5 71.8 reduce-scatter.30
  1454.6 71.8 reduce-scatter.32
  1530.9 65.3 reduce-scatter.26
  1600.5 65.3 reduce-scatter.24
  1670.1 65.4 reduce-scatter.22
where the time goes:
time: 1750 us; the launch traced here: 1740 us
  waiting for transfers between devices  1050 us (60%)
  matrix products  261 us (15%)
  local copies, waits for them, and re-layouts  170 us (10%)
  other arithmetic  161 us (9%)
  blocking collectives  77.5 us (4%)
    psum x1, waiting for transfers between devices, body(): ffn_full = lax.psum(project(hidden, down_weight), 'tensor')  200 us
    psum x1, waiting for transfers between devices, body(): branch = lax.psum(branch_part, 'tensor')  110 us
    psum x1, waiting for transfers between devices, body(): lax.psum(back_project(grad_gate, gate_weight) + back_project(grad_up, up_...  102 us
    reduce_scatter x1, waiting for transfers between devices, body(): lax.psum_scatter(up_grad, 'dp', scatter_dimension=0, tiled=True)  76.3 us
    reduce_scatter x1, waiting for transfers between devices, body(): lax.psum_scatter(down_grad, 'dp', scatter_dimension=1, tiled=True)  76.2 us
    reduce_scatter x1, waiting for transfers between devices, body(): lax.psum_scatter(gate_grad, 'dp', scatter_dimension=0, tiled=True)  76.2 us
    reduce_scatter x1, waiting for transfers between devices, body(): lax.psum_scatter(mamba_out_grad, 'dp', scatter_dimension=1, tiled=True)  69.7 us
    reduce_scatter x1, waiting for transfers between devices, body(): lax.psum_scatter(z_grad, 'dp', scatter_dimension=0, tiled=True)  69.7 us
  transfers between devices with their start and end apart: 15, of which 14 were waited for; matrix products, arithmetic and copies ran while one was open for 6% of the time, Pallas kernels for 0%

commit v1 on v0

--- a/solution.py
+++ b/solution.py
@@ -205,6 +205,34 @@
         one_block, (zeros_kv, zeros_kv), (offsets, log_totals)
     )
     return (query_grads.reshape(queries.shape), key_grad, value_grad)
+
+
+def dp_sum(row_split, col_split, vectors):
+    n_dp = lax.axis_size("dp")
+    pieces = [g.reshape(n_dp, -1) for g in row_split]
+    pieces += [
+        g.reshape(g.shape[0], n_dp, g.shape[1] // n_dp).transpose(1, 0, 2).reshape(n_dp, -1)
+        for g in col_split
+    ]
+    pieces += [jnp.broadcast_to(v.reshape(1, -1), (n_dp, v.size)) for v in vectors]
+    widths = [p.shape[1] for p in pieces]
+    lane_rows = -(-sum(widths) // 16384) * 128
+    pieces.append(jnp.zeros((n_dp, lane_rows * 128 - sum(widths)), jnp.float32))
+    packed = lax.psum_scatter(
+        jnp.concatenate(pieces, axis=1).reshape(n_dp * lane_rows, 128),
+        "dp",
+        scatter_dimension=0,
+        tiled=True,
+    ).reshape(-1)
+    shapes = [(g.shape[0] // n_dp, g.shape[1]) for g in row_split]
+    shapes += [(g.shape[0], g.shape[1] // n_dp) for g in col_split]
+    shapes += [v.shape for v in vectors]
+    outs = []
+    at = 0
+    for w, s in zip(widths, shapes):
+        outs.append(packed[at : at + w].reshape(s))
+        at += w
+    return outs
 
 
 def body(
@@ -362,21 +390,10 @@
     )
     grad_tokens_norm, norm_gain_grad = first_norm_back(grad_first)
     tokens_grad = (grad_middle + grad_tokens_norm).astype(jnp.bfloat16)
-    matrix_sums = (
-        lax.psum_scatter(query_grad, "dp", scatter_dimension=0, tiled=True),
-        lax.psum_scatter(key_grad, "dp", scatter_dimension=0, tiled=True),
-        lax.psum_scatter(value_grad, "dp", scatter_dimension=0, tiled=True),
-        lax.psum_scatter(attn_out_grad, "dp", scatter_dimension=1, tiled=True),
-        lax.psum_scatter(z_grad, "dp", scatter_dimension=0, tiled=True),
-        lax.psum_scatter(x_grad, "dp", scatter_dimension=0, tiled=True),
-        lax.psum_scatter(bc_grad_full, "dp", scatter_dimension=0, tiled=True),
-        lax.psum_scatter(dt_grad, "dp", scatter_dimension=0, tiled=True),
-        lax.psum_scatter(mamba_out_grad, "dp", scatter_dimension=1, tiled=True),
-        lax.psum_scatter(gate_grad, "dp", scatter_dimension=0, tiled=True),
-        lax.psum_scatter(up_grad, "dp", scatter_dimension=0, tiled=True),
-        lax.psum_scatter(down_grad, "dp", scatter_dimension=1, tiled=True),
-    )
-    vector_sums = lax.psum(
+    early = dp_sum((gate_grad, up_grad), (attn_out_grad, mamba_out_grad, down_grad), ())
+    late = dp_sum(
+        (query_grad, key_grad, value_grad, z_grad, x_grad, bc_grad_full, dt_grad),
+        (),
         (
             norm_gain_grad,
             conv_x_grad,
@@ -389,8 +406,22 @@
             mixer_gain_grad,
             ffn_gain_grad,
         ),
-        "dp",
-    )
+    )
+    matrix_sums = (
+        late[0],
+        late[1],
+        late[2],
+        early[2],
+        late[3],
+        late[4],
+        late[5],
+        late[6],
+        early[3],
+        early[0],
+        early[1],
+        early[4],
+    )
+    vector_sums = late[7:]
     return (
         block_output,
         tokens_grad,

time: 1750 us -> 1340 us (0.77)
  waiting for transfers between devices: 1050 us -> 593 us
  local copies, waits for them, and re-layouts: 170 us -> 314 us
  blocking collectives: 77.5 us -> 16.7 us
  matrix products: 261 us -> 236 us
    reduce_scatter x11 -> x2, waiting for transfers between devices: 629 us -> 251 us  [dp_sum(): lax.psum_scatter(jnp.concatenate(pieces, axis=1).reshape(n_dp * lane_rows...]
    reshape x0 -> x29, local copies, waits for them, and re-layouts: none -> 79.2 us  [the longest x2 29.3 us: dp_sum(): jnp.concatenate(pieces, axis=1).reshape(n_dp * lane_rows, 128)]
    psum x1 -> x0, blocking collectives: 61.6 us -> none  [body(): lax.psum((norm_gain_grad, conv_x_grad, conv_x_bias_grad, conv_bc_grad, co...]
    psum x1, waiting for transfers between devices: 200 us -> 159 us  [body(): ffn_full = lax.psum(project(hidden, down_weight), 'tensor')]
    unnamed x357 -> x395, local copies, waits for them, and re-layouts: 30.1 us -> 67 us
    psum x1, waiting for transfers between devices: 102 us -> 77.4 us  [body(): lax.psum(back_project(grad_gate, gate_weight) + back_project(grad_up, up_...]
    dot_general x10 -> x11, matrix products: 44.3 us -> 37 us  [outer_rows(): lax.dot_general(left, right, (((0,), (0,)), ((), ())), preferred_element_...]
  transfers between devices with their start and end apart: 15 -> 5, of which waited for: 14 -> 5; matrix products, arithmetic and copies ran while one was open for 6% -> 11% of each run, Pallas kernels for 0% -> 0%
where the time goes in v1:
time: 1340 us; the launch traced here: 1330 us
  waiting for transfers between devices  593 us (44%)
  local copies, waits for them, and re-layouts  314 us (23%)
  matrix products  236 us (18%)
  other arithmetic  145 us (11%)
  blocking collectives  16.7 us (1%)
  between operations  16.6 us (1%)
    reduce_scatter x2, waiting for transfers between devices, dp_sum(): lax.psum_scatter(jnp.concatenate(pieces, axis=1).reshape(n_dp * lane_rows...  251 us
    psum x1, waiting for transfers between devices, body(): ffn_full = lax.psum(project(hidden, down_weight), 'tensor')  159 us
    psum x1, waiting for transfers between devices, body(): branch = lax.psum(branch_part, 'tensor')  105 us
    psum x1, waiting for transfers between devices, body(): lax.psum(back_project(grad_gate, gate_weight) + back_project(grad_up, up_...  77.4 us
    unnamed x395, local copies, waits for them, and re-layouts  67 us
    dot_general x3, matrix products, mamba_core(): jnp.einsum('ctsh,cshp->cthp', intersection[..., None] * mixing, scaled, p...  37.9 us
    dynamic_slice x48, local copies, waits for them, and re-layouts, mamba_core(): lax.scan(advance, start_state, (pieces, decays, carry_on))  37 us
    dot_general x11, matrix products, outer_rows(): lax.dot_general(left, right, (((0,), (0,)), ((), ())), preferred_element_...  37 us
  transfers between devices with their start and end apart: 5, of which 5 were waited for; matrix products, arithmetic and copies ran while one was open for 11% of the time, Pallas kernels for 0%

profile of v1, /device:TPU:0, one launch (start us, length us, event | category | flops | bytes accessed | tf_op | source)
XLA Modules:
  0.0 1331.3 jit_solution(8452217001882804821)
XLA Ops:
  64.4 65.6 %while.63 = (s32[]{:T(128)}, f32[12,128,64]{2,1,0:T(8,128)S(1)}, f32[8,12,128,64]{3,2,1,0:T(8,128)}, f32[8,12,1,1]{1,3,2,0:T(1,128)}, f32[8,12]{1,0:T(8,128)}, /...) while((s32[]{:T(128)}, f32[12,128,64]{2,1,0:T(8,128)S(1)}, ...), condition=%wide.region_11.12_spmd.clone, body=%wide.region_10.11_spmd.clone.sunk | while | flops 589827 | bytes 3933984 | solution.py:119
  130.0 6.5 copy.181
  140.9 13.7 %multiply_reduce_fusion.13 = (f32[8,128]{1,0:T(8,128)S(1)}, f32[8,128,12,64]{1,3,2,0:T(8,128)S(1)}, f32[8,128,12,64]{1,3,2,0:T(8,128)}) fusion(f32[8,128,12,64]{1,0,3,2:T(8,128)S(1)} %bitcast.573, f32[8,128,12,64]{1,0,3,2:T(8,128)S(1)} %bitcast.560, f32[12]{0:T(128)S(1)} %copy-done.173, f32[8,128,12,64]{1,3,2,0:T(8,128)S(1)} %bitcast.575, ...), kind=kOutput, calls=%fused_computation.163 | convolution fusion | flops 1222114304 | bytes 16420912 | tf_op jit(solution)/shard_map/jvp(ctsh,cshp->cthp)/dot_general | solution.py:106
  174.8 24.1 %while.62 = (s32[]{:T(128)}, bf16[2,512,1,4,64]{1,4,3,2,0:T(8,128)(2,1)}, f32[2,1,4,512]{3,2,1,0:T(4,128)S(1)}, s32[2]{0:T(128)S(1)}, s32[1024]{0:T(1024)S(1)}, ...) while((s32[]{:T(128)}, ...), condition=%wide.region_8.9_spmd.clone, body=%wide.region_5.8_spmd.clone.sunk | while | flops 563608064 | bytes 32585968 | solution.py:158
  213.4 104.6 %all-reduce.34.cloned.1.call-done = f32[1024,1024]{1,0:T(8,128)} async-done(((f32[1024,1024]{1,0:T(8,128)}), f32[1024,1024]{1,0:T(8,128)}) %all-reduce.34.cloned.1.call-update) | async-done | bytes 4194320 | tf_op jit(solution)/shard_map/psum | solution.py:315
  372.0 7.0 copy.219
  389.7 77.4 %all-reduce.36.cloned.1.call-done = f32[1024,1024]{1,0:T(8,128)} async-done(((f32[1024,1024]{1,0:T(8,128)}), f32[1024,1024]{1,0:T(8,128)}) %all-reduce.36.cloned.1.call-update) | async-done | bytes 4194320 | tf_op jit(solution)/shard_map/psum | solution.py:334
  486.2 7.6 multiply_reduce_fusion.4
  506.4 14.9 %fusion.94 = (f32[8,128,12]{1,2,0:T(8,128)S(1)}, f32[8,128,12]{1,2,0:T(8,128)}, f32[8,128,128]{2,1,0:T(8,128)}) fusion(f32[8,128,12]{1,2,0:T(8,128)S(1)} %copy-done.114, f32[8,128,128]{2,1,0:T(8,128)S(1)} %copy-done.92, pred[128,128]{1,0:T(8,128)(4,1)S(1)} %copy-done.144, f32[8,128,12,64]{1,0,3,2:T(8,128)S(1)} %bitcast.561, ...), kind=kOutput, calls=%fused_computation.131 | convolution fusion | flops 1222746112 | bytes 7553024 | tf_op jit(solution)/shard_map/transpose(jvp(ctsh,cshp->cthp))/dot_general | solution.py:106
  527.9 45.0 %while.65 = (s32[]{:T(128)}, f32[12,128,64]{2,1,0:T(8,128)S(1)}, f32[8,12,128,64]{3,2,1,0:T(8,128)}, f32[8,12]{1,0:T(8,128)S(1)}, f32[8,12,128,64]{2,3,1,0:T(8,1...) while((s32[]{:T(128)}, f32[12,128,64]{2,1,0:T(8,128)S(1)}, ...), condition=%wide.region_26.27_spmd.clone, body=%wide.region_24.26_spmd.clone.sunk | while | flops 688120 | bytes 4325840 | solution.py:119
  572.9 7.5 fusion.73
  580.5 11.2 fusion.156
  591.7 11.4 fusion.153
  603.1 9.4 multiply_reduce_fusion.9
  652.5 65.9 %while.64 = (s32[]{:T(128)}, f32[1024,1,64]{0,2,1:T(8,128)S(1)}, f32[1024,1,64]{0,2,1:T(8,128)S(1)}, f32[2,512,1,4,64]{1,0,4,3,2:T(2,128)}, s32[2]{0:T(128)S(1)}...) while((s32[]{:T(128)}, f32[1024,1,64]{0,2,1:T(8,128)S(1)}, ...), condition=%wide.region_21.22_spmd.clone, body=%wide.region_19.21_spmd.clone.sunk | while | flops 1375664640 | bytes 120527144 | solution.py:204
  675.3 10.4 dynamic_update_slice.61
  707.9 10.4 dynamic_update_slice.61
  770.7 11.3 add_add_fusion.2
  788.6 16.0 %reshape.841 = f32[32768,128]{1,0:T(8,128)} reshape(f32[16,262144]{1,0:T(8,128)} %constant_dynamic-update-slice_fusion.12) | data formatting | bytes 33554432 | tf_op jit(solution)/shard_map/reshape | solution.py:222
  843.7 159.3 %all-reduce.38.cloned.1.call-done = (f32[1024,1024]{1,0:T(8,128)}, f32[1024,1024]{1,0:T(8,128)}, f32[16,16384]{1,0:T(8,128)}) async-done(((f32[1024,1024]{1,0:T(8,128)}, f32[1024,1024]{1,0:T(8,128)}, f32[16,16384]{1,0:T(8,128)}), (f32[1024,1024]{1,0:T(8,128)}, f32[1024,1024]{1,0:T(8,128)}, f32[16,16384]{1,0:T(8,128)})) %all-reduce.38.cloned.1.call-update) | async-done | bytes 9437200 | tf_op jit(solution)/shard_map/psum | solution.py:323
  1024.2 13.3 reshape.831
  1038.3 10.1 fusion.89
  1048.3 136.0 %reduce-scatter.5.cloned.1.call-done = f32[2048,128]{1,0:T(8,128)} async-done(((f32[32768,128]{1,0:T(8,128)}), f32[2048,128]{1,0:T(8,128)}) %reduce-scatter.5.cloned.1.call-update) | async-done | bytes 1048592 | tf_op jit(solution)/shard_map/reduce_scatter | solution.py:221
  1191.6 115.3 %reduce-scatter.3.cloned.1.call-done = f32[1280,128]{1,0:T(8,128)} async-done(((f32[20480,128]{1,0:T(8,128)}), f32[1280,128]{1,0:T(8,128)}) %reduce-scatter.3.cloned.1.call-update) | async-done | bytes 655376 | tf_op jit(solution)/shard_map/reduce_scatter | solution.py:221
  (777 shorter events, 552.7 us)
Async XLA Ops:
  7.2 322.4 %copy-start = (bf16[1024,1024]{1,0:T(8,128)(2,1)S(1)}, bf16[1024,1024]{1,0:T(8,128)(2,1)}, u32[]{:S(2)}) copy-start(bf16[1024,1024]{1,0:T(8,128)(2,1)} %param.57) | copy-start | bytes 6291460
  7.2 310.8 %all-reduce.34.cloned.1.call-start = ((), (), s32[]{:S(2)}) async-start(), calls=%async_computation.2 | async-start | bytes 8388608 | tf_op jit(solution)/shard_map/psum | solution.py:315
  16.3 36.9 %copy-start.38 = (f32[8,128,12]{2,0,1:T(8,128)}, f32[8,128,12]{2,0,1:T(8,128)S(1)}, u32[]{:S(2)}) copy-start(f32[8,128,12]{2,0,1:T(8,128)S(1)} %fusion.180) | copy-start | bytes 147460
  16.9 123.9 %copy-start.77 = (f32[8,128,12]{1,2,0:T(8,128)}, f32[8,128,12]{1,2,0:T(8,128)S(1)}, u32[]{:S(2)}) copy-start(f32[8,128,12]{1,2,0:T(8,128)S(1)} %copy.174) | copy-start | bytes 147460
  17.8 123.0 %copy-start.143 = (pred[128,128]{1,0:T(8,128)(4,1)}, pred[128,128]{1,0:T(8,128)(4,1)S(1)}, u32[]{:S(2)}) copy-start(pred[128,128]{1,0:T(8,128)(4,1)S(1)} %iota_compare_fusion.2) | copy-start | bytes 49156
  18.4 154.7 %copy-start.155 = (f32[32]{0:T(128)}, f32[32]{0:T(128)S(1)}, u32[]{:S(2)}) copy-start(f32[32]{0:T(128)S(1)} %multiply_power_fusion) | copy-start | bytes 388
  32.3 140.8 %copy-start.111 = (f32[1024]{0:T(1024)}, f32[1024]{0:T(1024)S(1)}, u32[]{:S(2)}) copy-start(f32[1024]{0:T(1024)S(1)} %get-tuple-element.762) | copy-start | bytes 12292
  32.3 17.8 %copy-start.101 = (f32[1024]{0:T(1024)}, f32[1024]{0:T(1024)S(1)}, u32[]{:S(2)}) copy-start(f32[1024]{0:T(1024)S(1)} %get-tuple-element.759) | copy-start | bytes 12292
  32.3 17.8 %copy-start.103 = (f32[1024]{0:T(1024)}, f32[1024]{0:T(1024)S(1)}, u32[]{:S(2)}) copy-start(f32[1024]{0:T(1024)S(1)} %get-tuple-element.760) | copy-start | bytes 12292
  32.4 440.0 %copy-start.118 = (f32[1024]{0:T(1024)}, f32[1024]{0:T(1024)S(1)}, u32[]{:S(2)}) copy-start(f32[1024]{0:T(1024)S(1)} %get-tuple-element.758) | copy-start | bytes 12292
  174.7 26.1 %copy-start.135 = (f32[768]{0:T(1024)S(1)}, f32[768]{0:T(1024)}, u32[]{:S(2)}) copy-start(f32[768]{0:T(1024)} %param.52) | copy-start | bytes 9220
  208.2 258.9 %all-reduce.36.cloned.1.call-start = ((), (), s32[]{:S(2)}) async-start(), calls=%async_computation.3 | async-start | bytes 8388608 | tf_op jit(solution)/shard_map/psum | solution.py:334
  321.8 150.5 %copy-start.109 = (f32[1024]{0:T(1024)}, f32[1024]{0:T(1024)S(1)}, u32[]{:S(2)}) copy-start(f32[1024]{0:T(1024)S(1)} %fusion.219) | copy-start | bytes 12292
  359.0 644.0 %all-reduce.38.cloned.1.call-start = ((), (), s32[]{:S(2)}) async-start(), calls=%async_computation.6 | async-start | bytes 18874368 | tf_op jit(solution)/shard_map/psum | solution.py:323
  527.9 45.0 %copy-start.44 = (bf16[1024,128]{1,0:T(8,128)(2,1)S(1)}, bf16[1024,128]{1,0:T(8,128)(2,1)}, u32[]{:S(2)}) copy-start(bf16[1024,128]{1,0:T(8,128)(2,1)} %get-tuple-element.747) | copy-start | bytes 786436
  527.9 52.6 %copy-start.80 = (f32[8,128,12]{1,2,0:T(8,128)S(1)}, f32[8,128,12]{1,2,0:T(8,128)}, u32[]{:S(2)}) copy-start(f32[8,128,12]{1,2,0:T(8,128)} %copy-done.79) | copy-start | bytes 147460
  572.9 18.8 %slice-start = ((s8[6291456]{0:T(1024)(128)(4,1)}), s8[4194304]{0:T(1024)(128)(4,1)S(1)}, s32[]{:S(2)}) async-start(s8[6291456]{0:T(1024)(128)(4,1)} %bitcast.551), calls=%async_computation.7 | async-start | bytes 8388608
  652.5 65.9 %copy-start.88 = (bf16[1024,64]{0,1:T(8,128)(2,1)S(1)}, bf16[1024,64]{0,1:T(8,128)(2,1)}, u32[]{:S(2)}) copy-start(bf16[1024,64]{0,1:T(8,128)(2,1)} %param.39) | copy-start | bytes 393220
  782.0 402.3 %reduce-scatter.5.cloned.1.call-start = ((), (), s32[]{:S(2)}) async-start(), calls=%async_computation.5 | async-start | bytes 17825792 | tf_op jit(solution)/shard_map/reduce_scatter | solution.py:221
  804.6 502.3 %reduce-scatter.3.cloned.1.call-start = ((), (), s32[]{:S(2)}) async-start(), calls=%async_computation.4 | async-start | bytes 11141120 | tf_op jit(solution)/shard_map/reduce_scatter | solution.py:221
  841.8 164.1 %copy-start.16 = (bf16[1024,1024]{1,0:T(8,128)(2,1)S(1)}, bf16[1024,1024]{1,0:T(8,128)(2,1)}, u32[]{:S(2)}) copy-start(bf16[1024,1024]{1,0:T(8,128)(2,1)} %param.33) | copy-start | bytes 6291460
  841.8 164.1 %copy-start.121 = (f32[1024]{0:T(1024)S(1)}, f32[1024]{0:T(1024)}, u32[]{:S(2)}) copy-start(f32[1024]{0:T(1024)} %copy-done.120) | copy-start | bytes 12292
  841.8 164.1 %copy-start.134 = (f32[1024]{0:T(1024)S(1)}, f32[1024]{0:T(1024)}, u32[]{:S(2)}) copy-start(f32[1024]{0:T(1024)} %param.36) | copy-start | bytes 12292
  1187.0 137.2 %copy-start.1 = (bf16[1024,1024]{1,0:T(8,128)(2,1)S(1)}, bf16[1024,1024]{1,0:T(8,128)(2,1)}, u32[]{:S(2)}) copy-start(bf16[1024,1024]{1,0:T(8,128)(2,1)} %param.57) | copy-start | bytes 6291460
  (168 other events, 769.0 us)
Sparse Core Ops, SparseCore 0:
  208.3 109.7 all-reduce.33
  359.2 107.9 all-reduce.35
  782.1 220.8 all-reduce.37
  1007.0 177.3 reduce-scatter.4
  1188.2 118.5 reduce-scatter.2

commit v2 on v1

--- a/solution.py
+++ b/solution.py
@@ -205,6 +205,13 @@
         one_block, (zeros_kv, zeros_kv), (offsets, log_totals)
     )
     return (query_grads.reshape(queries.shape), key_grad, value_grad)
+
+
+def tensor_sum(values):
+    if lax.axis_size("tensor") != 2:
+        return lax.psum(values, "tensor")
+    swapped = lax.ppermute(values, "tensor", perm=[(0, 1), (1, 0)])
+    return jax.tree.map(lambda mine, theirs: mine + theirs, values, swapped)
 
 
 def dp_sum(row_split, col_split, vectors):
@@ -312,7 +319,7 @@
     normed_gated = gated_wide * group_scale
     mixed = (normed_gated * mixer_gain[None, :]).astype(jnp.bfloat16)
     branch_part = project(attended, attn_out_weight) + project(mixed, mamba_out_weight)
-    branch = lax.psum(branch_part, "tensor")
+    branch = tensor_sum(branch_part)
     middle = tokens_wide + valid_col * branch
     second_wide, second_norm_back = jax.vjp(rms_norm, middle, ffn_gain)
     second_in = second_wide.astype(jnp.bfloat16)
@@ -320,7 +327,7 @@
     up_values = project(second_in, up_weight)
     hidden_wide, hidden_back = jax.vjp(swiglu, gate_values, up_values)
     hidden = hidden_wide.astype(jnp.bfloat16)
-    ffn_full = lax.psum(project(hidden, down_weight), "tensor")
+    ffn_full = tensor_sum(project(hidden, down_weight))
     block_output = (middle + valid_col * ffn_full).astype(jnp.bfloat16)
     cot_wide = cotangent.astype(jnp.float32)
     grad_ffn = (valid_col * cot_wide).astype(jnp.bfloat16)
@@ -331,8 +338,8 @@
     grad_up = grad_up_wide.astype(jnp.bfloat16)
     gate_grad = outer_rows(second_in, grad_gate)
     up_grad = outer_rows(second_in, grad_up)
-    grad_second = lax.psum(
-        back_project(grad_gate, gate_weight) + back_project(grad_up, up_weight), "tensor"
+    grad_second = tensor_sum(
+        back_project(grad_gate, gate_weight) + back_project(grad_up, up_weight)
     )
     grad_middle_norm, ffn_gain_grad = second_norm_back(grad_second)
     grad_middle = cot_wide + grad_middle_norm
@@ -385,8 +392,8 @@
             grad_bc_lin, bc_weight.astype(jnp.float32), (((1,), (1,)), ((), ())), precision=PRECISE
         )
     )
-    grad_first, bc_grad_full, conv_bc_grad, conv_bc_bias_grad = lax.psum(
-        (grad_first_part, bc_part, conv_bc_part, conv_bc_bias_part), "tensor"
+    grad_first, bc_grad_full, conv_bc_grad, conv_bc_bias_grad = tensor_sum(
+        (grad_first_part, bc_part, conv_bc_part, conv_bc_bias_part)
     )
     grad_tokens_norm, norm_gain_grad = first_norm_back(grad_first)
     tokens_grad = (grad_middle + grad_tokens_norm).astype(jnp.bfloat16)

time: 1340 us -> 1290 us (0.963)
  waiting for transfers between devices: 593 us -> 512 us
  other arithmetic: 145 us -> 159 us
    psum x3 -> x0, waiting for transfers between devices: 341 us -> none  [the longest x1 159 us: body(): ffn_full = lax.psum(project(hidden, down_weight), 'tensor')]
    ppermute x0 -> x7, waiting for transfers between devices: none -> 311 us  [tensor_sum(): swapped = lax.ppermute(values, 'tensor', perm=[(0, 1), (1, 0)])]
    reduce_scatter x2, waiting for transfers between devices: 251 us -> 201 us  [dp_sum(): lax.psum_scatter(jnp.concatenate(pieces, axis=1).reshape(n_dp * lane_rows...]
    unnamed x395 -> x391, local copies, waits for them, and re-layouts: 67 us -> 86.5 us
  transfers between devices with their start and end apart: 5 -> 9, of which waited for: 5 -> 6; matrix products, arithmetic and copies ran while one was open for 11% -> 13% of each run, Pallas kernels for 0% -> 0%
where the time goes in v2:
time: 1290 us; the launch traced here: 1270 us
  waiting for transfers between devices  512 us (40%)
  local copies, waits for them, and re-layouts  320 us (25%)
  matrix products  237 us (18%)
  other arithmetic  159 us (12%)
  between operations  16.5 us (1%)
    ppermute x7, waiting for transfers between devices, tensor_sum(): swapped = lax.ppermute(values, 'tensor', perm=[(0, 1), (1, 0)])  311 us
    reduce_scatter x2, waiting for transfers between devices, dp_sum(): lax.psum_scatter(jnp.concatenate(pieces, axis=1).reshape(n_dp * lane_rows...  201 us
    unnamed x391, local copies, waits for them, and re-layouts  86.5 us
    dot_general x11, matrix products, outer_rows(): lax.dot_general(left, right, (((0,), (0,)), ((), ())), preferred_element_...  37.7 us
    dynamic_slice x48, local copies, waits for them, and re-layouts, mamba_core(): lax.scan(advance, start_state, (pieces, decays, carry_on))  37.1 us
    dot_general x3, matrix products, mamba_core(): jnp.einsum('ctsh,cshp->cthp', intersection[..., None] * mixing, scaled, p...  36.9 us
    dot_general x11, matrix products, back_project(): lax.dot_general(grad_rows, weight, (((1,), (1,)), ((), ())), preferred_el...  33.2 us
    dot_general x12, matrix products, project(): return jnp.dot(left, right, preferred_element_type=jnp.float32)  31.8 us
  transfers between devices with their start and end apart: 9, of which 6 were waited for; matrix products, arithmetic and copies ran while one was open for 13% of the time, Pallas kernels for 0%

profile of v2, /device:TPU:0, one launch (start us, length us, event | category | flops | bytes accessed | tf_op | source)
XLA Modules:
  0.0 1272.6 jit_solution(1621479650953750727)
XLA Ops:
  67.7 54.7 %while.63 = (s32[]{:T(128)}, f32[12,128,64]{2,1,0:T(8,128)S(1)}, f32[8,12,128,64]{3,2,1,0:T(8,128)}, f32[8,12,1,1]{1,3,2,0:T(1,128)}, f32[8,12]{1,0:T(8,128)S(1)...) while((s32[]{:T(128)}, f32[12,128,64]{2,1,0:T(8,128)S(1)}, ...), condition=%wide.region_11.12_spmd.clone, body=%wide.region_10.11_spmd.clone.sunk | while | flops 589827 | bytes 3933520 | solution.py:119
  133.0 13.9 %multiply_reduce_fusion.13 = (f32[8,128]{1,0:T(8,128)S(1)}, f32[8,128,12,64]{1,3,2,0:T(8,128)S(1)}, f32[8,128,12,64]{1,3,2,0:T(8,128)}) fusion(f32[8,128,12,64]{1,0,3,2:T(8,128)S(1)} %bitcast.574, f32[8,128,12,64]{1,0,3,2:T(8,128)S(1)} %bitcast.561, f32[12]{0:T(128)S(1)} %copy-done.171, f32[8,128,12,64]{1,3,2,0:T(8,128)S(1)} %bitcast.576, ...), kind=kOutput, calls=%fused_computation.163 | convolution fusion | flops 1222114304 | bytes 16420912 | tf_op jit(solution)/shard_map/jvp(ctsh,cshp->cthp)/dot_general | solution.py:106
  166.6 25.7 %while.62 = (s32[]{:T(128)}, bf16[2,512,1,4,64]{1,4,3,2,0:T(8,128)(2,1)}, f32[2,1,4,512]{3,2,1,0:T(4,128)}, s32[2]{0:T(128)}, s32[1024]{0:T(1024)S(1)}, /*index=...) while((s32[]{:T(128)}, ...), condition=%wide.region_8.9_spmd.clone, body=%wide.region_5.8_spmd.clone.sunk | while | flops 563608064 | bytes 32717096 | solution.py:158
  215.1 78.1 %collective-permute-done = f32[1024,1024]{0,1:T(8,128)} collective-permute-done((f32[1024,1024]{0,1:T(8,128)}, f32[1024,1024]{0,1:T(8,128)}, u32[]{:S(2)}, u32[]{:S(2)}) %collective-permute-start) | collective-permute-done | bytes 4194336 | tf_op jit(solution)/shard_map/ppermute | solution.py:213
  348.2 69.8 %collective-permute-done.2 = f32[1024,1024]{0,1:T(8,128)} collective-permute-done((f32[1024,1024]{0,1:T(8,128)}, f32[1024,1024]{0,1:T(8,128)}, u32[]{:S(2)}, u32[]{:S(2)}) %collective-permute-start.2) | collective-permute-done | bytes 4194336 | tf_op jit(solution)/shard_map/ppermute | solution.py:213
  423.6 81.5 %collective-permute-done.1 = f32[1024,1024]{0,1:T(8,128)} collective-permute-done((f32[1024,1024]{0,1:T(8,128)}, f32[1024,1024]{0,1:T(8,128)}, u32[]{:S(2)}, u32[]{:S(2)}) %collective-permute-start.1) | collective-permute-done | bytes 4194336 | tf_op jit(solution)/shard_map/ppermute | solution.py:213
  505.1 9.4 multiply_convert_fusion
  525.9 7.6 multiply_reduce_fusion.4
  546.7 14.9 %fusion.94 = (f32[8,128,12]{1,2,0:T(8,128)}, f32[8,128,12]{1,2,0:T(8,128)}, f32[8,128,128]{2,1,0:T(8,128)}) fusion(f32[8,128,12]{1,2,0:T(8,128)S(1)} %copy-done.108, f32[8,128,128]{2,1,0:T(8,128)S(1)} %copy-done.83, pred[128,128]{1,0:T(8,128)(4,1)S(1)} %copy-done.145, f32[8,128,12,64]{1,0,3,2:T(8,128)S(1)} %bitcast.562, f32[8,128,12]{1,2,0:T(8,128)S(1)} %copy-done.67, ...), kind=kOutput, calls=%fused_computation.131 | convolution fusion | flops 1222746112 | bytes 7553024 | tf_op jit(solution)/shard_map/transpose(jvp(ctsh,cshp->cthp))/dot_general | solution.py:106
  568.4 45.2 %while.65 = (s32[]{:T(128)}, f32[12,128,64]{2,1,0:T(8,128)S(1)}, f32[8,12,128,64]{3,2,1,0:T(8,128)}, f32[8,12]{1,0:T(8,128)S(1)}, f32[8,12,128,64]{2,3,1,0:T(8,1...) while((s32[]{:T(128)}, f32[12,128,64]{2,1,0:T(8,128)S(1)}, ...), condition=%wide.region_23.24_spmd.clone, body=%wide.region_21.23_spmd.clone.sunk | while | flops 688120 | bytes 4325840 | solution.py:119
  613.7 9.8 fusion.73
  623.5 11.6 fusion.160
  635.2 11.1 fusion.157
  646.4 66.8 %while.64 = (s32[]{:T(128)}, f32[1024,1,64]{0,2,1:T(8,128)S(1)}, f32[1024,1,64]{0,2,1:T(8,128)}, f32[2,512,1,4,64]{1,0,4,3,2:T(2,128)}, s32[2]{0:T(128)S(1)}, /*...) while((s32[]{:T(128)}, f32[1024,1,64]{0,2,1:T(8,128)S(1)}, ...), condition=%wide.region_18.19_spmd.clone, body=%wide.region_16.18_spmd.clone.sunk | while | flops 1375664640 | bytes 120527144 | solution.py:204
  669.4 10.3 dynamic_update_slice.61
  702.7 10.3 dynamic_update_slice.61
  742.4 8.1 multiply_reduce_fusion.9
  798.5 9.6 add_add_fusion.2
  838.0 81.5 %collective-permute-done.6 = f32[256]{0:T(256)S(1)} collective-permute-done((f32[256]{0:T(256)S(1)}, f32[256]{0:T(256)S(1)}, u32[]{:S(2)}, u32[]{:S(2)}) %collective-permute-start.6) | collective-permute-done | bytes 1056 | tf_op jit(solution)/shard_map/ppermute | solution.py:213
  945.2 11.2 reshape.831
  963.6 7.5 copy.264
  1008.8 15.7 %reshape.841 = f32[32768,128]{1,0:T(8,128)} reshape(f32[16,262144]{1,0:T(8,128)} %constant_dynamic-update-slice_fusion.12) | data formatting | bytes 33554432 | tf_op jit(solution)/shard_map/reshape | solution.py:229
  1039.8 37.1 %reduce-scatter.3.cloned.1.call-done = f32[1280,128]{1,0:T(8,128)} async-done(((f32[20480,128]{1,0:T(8,128)}), f32[1280,128]{1,0:T(8,128)}) %reduce-scatter.3.cloned.1.call-update) | async-done | bytes 655376 | tf_op jit(solution)/shard_map/reduce_scatter | solution.py:228
  1094.5 163.5 %reduce-scatter.5.cloned.1.call-done = f32[2048,128]{1,0:T(8,128)} async-done(((f32[32768,128]{1,0:T(8,128)}), f32[2048,128]{1,0:T(8,128)}) %reduce-scatter.5.cloned.1.call-update) | async-done | bytes 1048592 | tf_op jit(solution)/shard_map/reduce_scatter | solution.py:228
  (787 shorter events, 584.2 us)
Async XLA Ops:
  7.2 296.7 %copy-start = (bf16[1024,1024]{1,0:T(8,128)(2,1)S(1)}, bf16[1024,1024]{1,0:T(8,128)(2,1)}, u32[]{:S(2)}) copy-start(bf16[1024,1024]{1,0:T(8,128)(2,1)} %param.55) | copy-start | bytes 6291460
  7.2 1069.8 %reduce-scatter.3.cloned.1.call-start = ((), (), s32[]{:S(2)}) async-start(), calls=%async_computation.2 | async-start | bytes 11141120 | tf_op jit(solution)/shard_map/reduce_scatter | solution.py:228
  19.8 113.1 %copy-start.66 = (f32[8,128,12]{1,2,0:T(8,128)}, f32[8,128,12]{1,2,0:T(8,128)S(1)}, u32[]{:S(2)}) copy-start(f32[8,128,12]{1,2,0:T(8,128)S(1)} %copy.210) | copy-start | bytes 147460
  21.8 143.4 %copy-start.157 = (f32[32]{0:T(128)}, f32[32]{0:T(128)S(1)}, u32[]{:S(2)}) copy-start(f32[32]{0:T(128)S(1)} %multiply_power_fusion) | copy-start | bytes 388
  22.8 142.4 %copy-start.105 = (f32[1024]{0:T(1024)}, f32[1024]{0:T(1024)S(1)}, u32[]{:S(2)}) copy-start(f32[1024]{0:T(1024)S(1)} %get-tuple-element.782) | copy-start | bytes 12292
  201.4 91.8 %collective-permute-start = (f32[1024,1024]{0,1:T(8,128)}, f32[1024,1024]{0,1:T(8,128)}, u32[]{:S(2)}, u32[]{:S(2)}) collective-permute-start(f32[1024,1024]{0,1:T(8,128)} %convolution_add_fusion), channel_id=1, source_target_pairs={{0,1},{1,0},{2,3},{3,2},{4,5},{5,4},{6,7},{7,6},{8,9},{9,8},{10,11... | collective-permute-start | bytes 12582920 | tf_op jit(solution)/shard_map/ppermute | solution.py:213
  212.7 80.5 %copy-start.13 = (bf16[1024,1024]{0,1:T(8,128)(2,1)S(1)}, bf16[1024,1024]{0,1:T(8,128)(2,1)}, u32[]{:S(2)}) copy-start(bf16[1024,1024]{0,1:T(8,128)(2,1)} %copy.207) | copy-start | bytes 6291460
  215.1 83.2 %copy-start.114 = (f32[1024]{0:T(1024)S(1)}, f32[1024]{0:T(1024)}, u32[]{:S(2)}) copy-start(f32[1024]{0:T(1024)} %param.54) | copy-start | bytes 12292
  324.3 93.8 %collective-permute-start.2 = (f32[1024,1024]{0,1:T(8,128)}, f32[1024,1024]{0,1:T(8,128)}, u32[]{:S(2)}, u32[]{:S(2)}) collective-permute-start(f32[1024,1024]{0,1:T(8,128)} %convolution_add_fusion.1), channel_id=1, source_target_pairs={{0,1},{1,0},{2,3},{3,2},{4,5},{5,4},{6,7},{7,6},{8,9},{9,8},{10,11... | collective-permute-start | bytes 12582920 | tf_op jit(solution)/shard_map/ppermute | solution.py:213
  330.6 174.4 %collective-permute-start.1 = (f32[1024,1024]{0,1:T(8,128)}, f32[1024,1024]{0,1:T(8,128)}, u32[]{:S(2)}, u32[]{:S(2)}) collective-permute-start(f32[1024,1024]{0,1:T(8,128)} %fusion.253), channel_id=1, source_target_pairs={{0,1},{1,0},{2,3},{3,2},{4,5},{5,4},{6,7},{7,6},{8,9},{9,8},{10,11... | collective-permute-start | bytes 12582920 | tf_op jit(solution)/shard_map/ppermute | solution.py:213
  343.6 74.4 %copy-start.18 = (f32[1024,1024]{0,1:T(8,128)S(1)}, f32[1024,1024]{0,1:T(8,128)}, u32[]{:S(2)}) copy-start(f32[1024,1024]{0,1:T(8,128)} %copy-done.17) | copy-start | bytes 12582916
  348.2 75.3 %copy-start.122 = (f32[1024]{0:T(1024)S(1)}, f32[1024]{0:T(1024)}, u32[]{:S(2)}) copy-start(f32[1024]{0:T(1024)} %copy-done.121) | copy-start | bytes 12292
  348.2 156.8 %copy-start.42 = (bf16[1024,1024]{0,1:T(8,128)(2,1)S(1)}, bf16[1024,1024]{0,1:T(8,128)(2,1)}, u32[]{:S(2)}) copy-start(bf16[1024,1024]{0,1:T(8,128)(2,1)} %copy.227) | copy-start | bytes 6291460
  423.5 90.9 %copy-start.31 = (f32[1024,768]{1,0:T(8,128)S(1)}, f32[1024,768]{1,0:T(8,128)}, u32[]{:S(2)}) copy-start(f32[1024,768]{1,0:T(8,128)} %copy.224) | copy-start | bytes 9437188
  423.5 90.9 %copy-start.130 = (f32[768]{0:T(1024)S(1)}, f32[768]{0:T(1024)}, u32[]{:S(2)}) copy-start(f32[768]{0:T(1024)} %param.52) | copy-start | bytes 9220
  423.6 90.9 %copy-start.135 = (f32[1024]{0:T(1024)S(1)}, f32[1024]{0:T(1024)}, u32[]{:S(2)}) copy-start(f32[1024]{0:T(1024)} %copy-done.134) | copy-start | bytes 12292
  423.6 90.9 %copy-start.166 = (bf16[768,1024]{1,0:T(8,128)(2,1)S(1)}, bf16[768,1024]{1,0:T(8,128)(2,1)}, u32[]{:S(2)}) copy-start(bf16[768,1024]{1,0:T(8,128)(2,1)} %param.53) | copy-start | bytes 4718596
  568.4 55.1 %copy-start.70 = (f32[8,128,12]{1,2,0:T(8,128)S(1)}, f32[8,128,12]{1,2,0:T(8,128)}, u32[]{:S(2)}) copy-start(f32[8,128,12]{1,2,0:T(8,128)} %copy-done.69) | copy-start | bytes 147460
  808.1 117.4 %collective-permute-start.3 = (f32[1024,1024]{0,1:T(8,128)}, f32[1024,1024]{0,1:T(8,128)}, u32[]{:S(2)}, u32[]{:S(2)}) collective-permute-start(f32[1024,1024]{0,1:T(8,128)} %add_add_fusion.2), channel_id=1, source_target_pairs={{0,1},{1,0},{2,3},{3,2},{4,5},{5,4},{6,7},{7,6},{8,9},{9,8},{10,11... | collective-permute-start | bytes 12582920 | tf_op jit(solution)/shard_map/ppermute | solution.py:213
  824.1 95.5 %collective-permute-start.4 = (f32[1024,256]{1,0:T(8,128)S(1)}, f32[1024,256]{1,0:T(8,128)}, u32[]{:S(2)}, u32[]{:S(2)}) collective-permute-start(f32[1024,256]{1,0:T(8,128)S(1)} %fusion.258), channel_id=1, source_target_pairs={{0,1},{1,0},{2,3},{3,2},{4,5},{5,4},{6,7},{7,6},{8,9},{9,8},{10,11... | collective-permute-start | bytes 3145736 | tf_op jit(solution)/shard_map/ppermute | solution.py:213
  824.7 94.8 %collective-permute-start.5 = (f32[4,256]{1,0:T(4,128)S(1)}, f32[4,256]{1,0:T(4,128)S(1)}, u32[]{:S(2)}, u32[]{:S(2)}) collective-permute-start(f32[4,256]{1,0:T(4,128)S(1)} %pad_add_fusion.1), channel_id=1, source_target_pairs={{0,1},{1,0},{2,3},{3,2},{4,5},{5,4},{6,7},{7,6},{8,9},{9,8},{10,11... | collective-permute-start | bytes 12296 | tf_op jit(solution)/shard_map/ppermute | solution.py:213
  826.3 93.2 %collective-permute-start.6 = (f32[256]{0:T(256)S(1)}, f32[256]{0:T(256)S(1)}, u32[]{:S(2)}, u32[]{:S(2)}) collective-permute-start(f32[256]{0:T(256)S(1)} %get-tuple-element.620), channel_id=1, source_target_pairs={{0,1},{1,0},{2,3},{3,2},{4,5},{5,4},{6,7},{7,6},{8,9},{9,8},{10,11... | collective-permute-start | bytes 3080 | tf_op jit(solution)/shard_map/ppermute | solution.py:213
  956.4 301.6 %reduce-scatter.5.cloned.1.call-start = ((), (), s32[]{:S(2)}) async-start(), calls=%async_computation.3 | async-start | bytes 17825792 | tf_op jit(solution)/shard_map/reduce_scatter | solution.py:228
  1093.1 172.2 %copy-start.1 = (bf16[1024,1024]{1,0:T(8,128)(2,1)S(1)}, bf16[1024,1024]{1,0:T(8,128)(2,1)}, u32[]{:S(2)}) copy-start(bf16[1024,1024]{1,0:T(8,128)(2,1)} %param.55) | copy-start | bytes 6291460
  (172 other events, 1049.9 us)
Sparse Core Ops, SparseCore 0:
  956.6 120.3 reduce-scatter.2
  1081.1 176.9 reduce-scatter.4

commit v3 on v2

--- a/solution.py
+++ b/solution.py
@@ -4,6 +4,7 @@
 import jax.numpy as jnp
 from jax import lax
 from jax.sharding import PartitionSpec as P
+
 
 SSM_HEADS = 24
 SSM_HEAD_DIM = 64
@@ -116,7 +117,7 @@
         return (decay_now[:, None, None] * entering + piece_now, entering)
 
     start_state = jnp.zeros((head_count, STATE, SSM_HEAD_DIM), jnp.float32)
-    final_state, entering = lax.scan(advance, start_state, (pieces, decays, carry_on))
+    _, entering = lax.scan(advance, start_state, (pieces, decays, carry_on))
     across = (
         jnp.einsum("ctn,chnp->cthp", read_keys, entering, precision=PRECISE)
         * jnp.exp(log_decay)[..., None]
@@ -328,7 +329,6 @@
     hidden_wide, hidden_back = jax.vjp(swiglu, gate_values, up_values)
     hidden = hidden_wide.astype(jnp.bfloat16)
     ffn_full = tensor_sum(project(hidden, down_weight))
-    block_output = (middle + valid_col * ffn_full).astype(jnp.bfloat16)
     cot_wide = cotangent.astype(jnp.float32)
     grad_ffn = (valid_col * cot_wide).astype(jnp.bfloat16)
     down_grad = outer_rows(hidden, grad_ffn)
@@ -339,7 +339,7 @@
     gate_grad = outer_rows(second_in, grad_gate)
     up_grad = outer_rows(second_in, grad_up)
     grad_second = tensor_sum(
-        back_project(grad_gate, gate_weight) + back_project(grad_up, up_weight)
+        back_project(grad_gate, gate_weight) + back_project(grad_up, up_weight),
     )
     grad_middle_norm, ffn_gain_grad = second_norm_back(grad_second)
     grad_middle = cot_wide + grad_middle_norm
@@ -396,6 +396,8 @@
         (grad_first_part, bc_part, conv_bc_part, conv_bc_bias_part)
     )
     grad_tokens_norm, norm_gain_grad = first_norm_back(grad_first)
+    ffn_late, middle_late, _ = lax.optimization_barrier((ffn_full, middle, grad_first))
+    block_output = (middle_late + valid_col * ffn_late).astype(jnp.bfloat16)
     tokens_grad = (grad_middle + grad_tokens_norm).astype(jnp.bfloat16)
     early = dp_sum((gate_grad, up_grad), (attn_out_grad, mamba_out_grad, down_grad), ())
     late = dp_sum(

time: 1290 us -> 1230 us (0.953)
  waiting for transfers between devices: 512 us -> 430 us
  matrix products: 237 us -> 250 us
    reduce_scatter x2, waiting for transfers between devices: 201 us -> 107 us  [dp_sum(): lax.psum_scatter(jnp.concatenate(pieces, axis=1).reshape(n_dp * lane_rows...]
    unnamed x391 -> x387, local copies, waits for them, and re-layouts: 86.5 us -> 75.7 us
  transfers between devices with their start and end apart: 9 -> 9, of which waited for: 6 -> 5; matrix products, arithmetic and copies ran while one was open for 13% -> 15% of each run, Pallas kernels for 0% -> 0%
where the time goes in v3:
time: 1230 us; the launch traced here: 1210 us
  waiting for transfers between devices  430 us (35%)
  local copies, waits for them, and re-layouts  329 us (27%)
  matrix products  250 us (20%)
  other arithmetic  160 us (13%)
  between operations  16.3 us (1%)
    ppermute x7, waiting for transfers between devices, tensor_sum(): swapped = lax.ppermute(values, 'tensor', perm=[(0, 1), (1, 0)])  323 us
    reduce_scatter x2, waiting for transfers between devices, dp_sum(): lax.psum_scatter(jnp.concatenate(pieces, axis=1).reshape(n_dp * lane_rows...  107 us
    unnamed x387, local copies, waits for them, and re-layouts  75.7 us
    dot_general x3, matrix products, mamba_core(): jnp.einsum('ctsh,cshp->cthp', intersection[..., None] * mixing, scaled, p...  37.9 us
    dynamic_slice x48, local copies, waits for them, and re-layouts, mamba_core(): _, entering = lax.scan(advance, start_state, (pieces, decays, carry_on))  37.4 us
    dot_general x12, matrix products, project(): return jnp.dot(left, right, preferred_element_type=jnp.float32)  37.3 us
    dot_general x11, matrix products, outer_rows(): lax.dot_general(left, right, (((0,), (0,)), ((), ())), preferred_element_...  37.3 us
    dot_general x11, matrix products, back_project(): lax.dot_general(grad_rows, weight, (((1,), (1,)), ((), ())), preferred_el...  36 us
  transfers between devices with their start and end apart: 9, of which 5 were waited for; matrix products, arithmetic and copies ran while one was open for 15% of the time, Pallas kernels for 0%

profile of v3, /device:TPU:0, one launch (start us, length us, event | category | flops | bytes accessed | tf_op | source)
XLA Modules:
  0.0 1214.9 jit_solution(4782520945741350305)
XLA Ops:
  27.7 9.9 fusion.138
  61.5 65.9 %while.63 = (s32[]{:T(128)}, f32[12,128,64]{2,1,0:T(8,128)S(1)}, f32[8,12,128,64]{3,2,1,0:T(8,128)}, f32[8,12,1,1]{1,3,2,0:T(1,128)}, f32[8,12]{1,0:T(8,128)}, /...) while((s32[]{:T(128)}, f32[12,128,64]{2,1,0:T(8,128)S(1)}, ...), condition=%wide.region_11.12_spmd.clone, body=%wide.region_10.11_spmd.clone.sunk | while | flops 589827 | bytes 3934992 | solution.py:120
  152.6 14.1 %multiply_reduce_fusion.13 = (f32[8,128]{1,0:T(8,128)S(1)}, f32[8,128,12,64]{1,3,2,0:T(8,128)S(1)}, f32[8,128,12,64]{1,3,2,0:T(8,128)}) fusion(f32[8,128,12,64]{1,0,3,2:T(8,128)S(1)} %bitcast.576, f32[8,128,12,64]{1,0,3,2:T(8,128)S(1)} %bitcast.562, f32[12]{0:T(128)S(1)} %copy-done.177, f32[8,128,12,64]{1,3,2,0:T(8,128)S(1)} %bitcast.575, ...), kind=kOutput, calls=%fused_computation.163 | convolution fusion | flops 1222114304 | bytes 16420912 | tf_op jit(solution)/shard_map/jvp(ctsh,cshp->cthp)/dot_general | solution.py:107
  186.4 25.8 %while.62 = (s32[]{:T(128)}, bf16[2,512,1,4,64]{1,4,3,2,0:T(8,128)(2,1)}, f32[2,1,4,512]{3,2,1,0:T(4,128)}, s32[2]{0:T(128)}, s32[1024]{0:T(1024)S(1)}, /*index=...) while((s32[]{:T(128)}, ...), condition=%wide.region_8.9_spmd.clone, body=%wide.region_5.8_spmd.clone.sunk | while | flops 563608064 | bytes 32717088 | solution.py:159
  235.2 78.0 %collective-permute-done = f32[1024,1024]{0,1:T(8,128)} collective-permute-done((f32[1024,1024]{0,1:T(8,128)}, f32[1024,1024]{0,1:T(8,128)}, u32[]{:S(2)}, u32[]{:S(2)}) %collective-permute-start) | collective-permute-done | bytes 4194336 | tf_op jit(solution)/shard_map/ppermute | solution.py:214
  365.6 86.5 %collective-permute-done.2 = f32[1024,1024]{0,1:T(8,128)S(1)} collective-permute-done((f32[1024,1024]{0,1:T(8,128)S(1)}, f32[1024,1024]{0,1:T(8,128)S(1)}, u32[]{:S(2)}, u32[]{:S(2)}) %collective-permute-start.2) | collective-permute-done | bytes 4194336 | tf_op jit(solution)/shard_map/ppermute | solution.py:214
  468.0 7.4 multiply_reduce_fusion.4
  488.4 11.0 fusion.157
  499.4 15.2 %fusion.94 = (f32[8,128,12]{1,2,0:T(8,128)}, f32[8,128,12]{1,2,0:T(8,128)}, f32[8,128,128]{2,1,0:T(8,128)}) fusion(f32[8,128,12]{1,2,0:T(8,128)S(1)} %copy-done.110, f32[8,128,128]{2,1,0:T(8,128)S(1)} %copy-done.87, pred[128,128]{1,0:T(8,128)(4,1)S(1)} %copy-done.144, f32[8,128,12,64]{1,0,3,2:T(8,128)S(1)} %bitcast.563, f32[8,128,12]{1,2,0:T(8,128)S(1)} %copy-done.71, ...), kind=kOutput, calls=%fused_computation.131 | convolution fusion | flops 1222746112 | bytes 7553024 | tf_op jit(solution)/shard_map/transpose(jvp(ctsh,cshp->cthp))/dot_general | solution.py:107
  521.4 45.4 %while.65 = (s32[]{:T(128)}, f32[12,128,64]{2,1,0:T(8,128)S(1)}, f32[8,12,128,64]{3,2,1,0:T(8,128)}, f32[8,12]{1,0:T(8,128)S(1)}, f32[8,12,128,64]{2,3,1,0:T(8,1...) while((s32[]{:T(128)}, f32[12,128,64]{2,1,0:T(8,128)S(1)}, ...), condition=%wide.region_23.24_spmd.clone, body=%wide.region_21.23_spmd.clone.sunk | while | flops 688120 | bytes 4325832 | solution.py:120
  566.8 15.1 %fusion.160 = f32[8,128,128]{2,1,0:T(8,128)} fusion(f32[8,12,128,64]{3,2,1,0:T(8,128)} %get-tuple-element.344, f32[8,128,12,64]{1,0,3,2:T(8,128)} %bitcast.561, f32[8,128,12]{1,2,0:T(8,128)S(1)} %copy-done.74, f32[8,128,12]{1,2,0:T(8,128)S(1)} %copy-done.71), kind=kOutput, calls=%fused_computation.222 | convolution fusion | flops 1209532416 | bytes 6914048 | tf_op jit(solution)/shard_map/transpose(jvp(csn,cshp->chnp))/dot_general | solution.py:111
  581.9 6.9 fusion.73
  590.3 69.9 %while.64 = (s32[]{:T(128)}, f32[1024,1,64]{0,2,1:T(8,128)}, f32[1024,1,64]{0,2,1:T(8,128)}, f32[2,512,1,4,64]{1,0,4,3,2:T(2,128)}, s32[2]{0:T(128)}, /*index=5*...) while((s32[]{:T(128)}, f32[1024,1,64]{0,2,1:T(8,128)}, ...), condition=%wide.region_18.19_spmd.clone, body=%wide.region_16.18_spmd.clone.sunk | while | flops 1375664640 | bytes 131537384 | solution.py:205
  605.4 10.4 dynamic_update_slice.61
  640.1 10.4 dynamic_update_slice.61
  679.4 8.7 multiply_reduce_fusion.9
  768.0 11.4 add_add_fusion.2
  795.0 72.1 %collective-permute-done.3 = f32[1024,1024]{0,1:T(8,128)} collective-permute-done((f32[1024,1024]{0,1:T(8,128)}, f32[1024,1024]{0,1:T(8,128)}, u32[]{:S(2)}, u32[]{:S(2)}) %collective-permute-start.3) | collective-permute-done | bytes 4194336 | tf_op jit(solution)/shard_map/ppermute | solution.py:214
  888.4 11.2 reshape.831
  906.8 7.3 copy.264
  914.2 7.0 reshape.840
  952.1 16.2 %reshape.841 = f32[32768,128]{1,0:T(8,128)} reshape(f32[16,262144]{1,0:T(8,128)} %constant_dynamic-update-slice_fusion.12) | data formatting | bytes 33554432 | tf_op jit(solution)/shard_map/reshape | solution.py:230
  973.7 86.0 %collective-permute-done.1 = f32[1024,1024]{0,1:T(8,128)S(1)} collective-permute-done((f32[1024,1024]{0,1:T(8,128)S(1)}, f32[1024,1024]{0,1:T(8,128)S(1)}, u32[]{:S(2)}, u32[]{:S(2)}) %collective-permute-start.1) | collective-permute-done | bytes 4194336 | tf_op jit(solution)/shard_map/ppermute | solution.py:214
  1093.7 107.0 %reduce-scatter.5.cloned.1.call-done = f32[2048,128]{1,0:T(8,128)} async-done(((f32[32768,128]{1,0:T(8,128)}), f32[2048,128]{1,0:T(8,128)}) %reduce-scatter.5.cloned.1.call-update) | async-done | bytes 1048592 | tf_op jit(solution)/shard_map/reduce_scatter | solution.py:229
  (815 shorter events, 597.8 us)
Async XLA Ops:
  7.2 316.7 %copy-start = (bf16[1024,1024]{1,0:T(8,128)(2,1)S(1)}, bf16[1024,1024]{1,0:T(8,128)(2,1)}, u32[]{:S(2)}) copy-start(bf16[1024,1024]{1,0:T(8,128)(2,1)} %param.55) | copy-start | bytes 6291460
  7.2 1069.0 %reduce-scatter.3.cloned.1.call-start = ((), (), s32[]{:S(2)}) async-start(), calls=%async_computation.2 | async-start | bytes 11141120 | tf_op jit(solution)/shard_map/reduce_scatter | solution.py:229
  17.4 134.2 %copy-start.70 = (f32[8,128,12]{1,2,0:T(8,128)}, f32[8,128,12]{1,2,0:T(8,128)S(1)}, u32[]{:S(2)}) copy-start(f32[8,128,12]{1,2,0:T(8,128)S(1)} %copy.210) | copy-start | bytes 147460
  27.5 157.5 %copy-start.105 = (f32[1024]{0:T(1024)}, f32[1024]{0:T(1024)S(1)}, u32[]{:S(2)}) copy-start(f32[1024]{0:T(1024)S(1)} %get-tuple-element.786) | copy-start | bytes 12292
  27.6 426.5 %copy-start.107 = (f32[1024]{0:T(1024)}, f32[1024]{0:T(1024)S(1)}, u32[]{:S(2)}) copy-start(f32[1024]{0:T(1024)S(1)} %get-tuple-element.782) | copy-start | bytes 12292
  221.4 91.8 %collective-permute-start = (f32[1024,1024]{0,1:T(8,128)}, f32[1024,1024]{0,1:T(8,128)}, u32[]{:S(2)}, u32[]{:S(2)}) collective-permute-start(f32[1024,1024]{0,1:T(8,128)} %convolution_add_fusion), channel_id=1, source_target_pairs={{0,1},{1,0},{2,3},{3,2},{4,5},{5,4},{6,7},{7,6},{8,9},{9,8},{10,11... | collective-permute-start | bytes 12582920 | tf_op jit(solution)/shard_map/ppermute | solution.py:214
  232.8 80.4 %copy-start.13 = (bf16[1024,1024]{0,1:T(8,128)(2,1)S(1)}, bf16[1024,1024]{0,1:T(8,128)(2,1)}, u32[]{:S(2)}) copy-start(bf16[1024,1024]{0,1:T(8,128)(2,1)} %copy.207) | copy-start | bytes 6291460
  235.2 83.1 %copy-start.115 = (f32[1024]{0:T(1024)S(1)}, f32[1024]{0:T(1024)}, u32[]{:S(2)}) copy-start(f32[1024]{0:T(1024)} %param.54) | copy-start | bytes 12292
  361.5 90.7 %copy-start.10 = (f32[1024,1024]{0,1:T(8,128)S(1)}, f32[1024,1024]{0,1:T(8,128)}, u32[]{:S(2)}) copy-start(f32[1024,1024]{0,1:T(8,128)} %copy-done.9) | copy-start | bytes 12582916
  361.5 90.6 %collective-permute-start.2 = (f32[1024,1024]{0,1:T(8,128)S(1)}, f32[1024,1024]{0,1:T(8,128)S(1)}, u32[]{:S(2)}, u32[]{:S(2)}) collective-permute-start(f32[1024,1024]{0,1:T(8,128)S(1)} %convolution_add_fusion.1), channel_id=1, source_target_pairs={{0,1},{1,0},{2,3},{3,2},{4,5},{5,4},{6,7},{7,6},{8,9},{9,8},{10,11... | collective-permute-start | bytes 12582920 | tf_op jit(solution)/shard_map/ppermute | solution.py:214
  365.6 88.5 %copy-start.121 = (f32[1024]{0:T(1024)S(1)}, f32[1024]{0:T(1024)}, u32[]{:S(2)}) copy-start(f32[1024]{0:T(1024)} %copy-done.120) | copy-start | bytes 12292
  365.6 88.5 %copy-start.41 = (bf16[1024,1024]{0,1:T(8,128)(2,1)S(1)}, bf16[1024,1024]{0,1:T(8,128)(2,1)}, u32[]{:S(2)}) copy-start(bf16[1024,1024]{0,1:T(8,128)(2,1)} %copy.227) | copy-start | bytes 6291460
  728.9 58.6 %collective-permute-start.6 = (f32[256]{0:T(256)}, f32[256]{0:T(256)}, u32[]{:S(2)}, u32[]{:S(2)}) collective-permute-start(f32[256]{0:T(256)} %get-tuple-element.624), channel_id=1, source_target_pairs={{0,1},{1,0},{2,3},{3,2},{4,5},{5,4},{6,7},{7,6},{8,9},{9,8},{10,11... | collective-permute-start | bytes 3080 | tf_op jit(solution)/shard_map/ppermute | solution.py:214
  731.0 57.2 %collective-permute-start.5 = (f32[4,256]{1,0:T(4,128)}, f32[4,256]{1,0:T(4,128)}, u32[]{:S(2)}, u32[]{:S(2)}) collective-permute-start(f32[4,256]{1,0:T(4,128)} %pad_add_fusion.1), channel_id=1, source_target_pairs={{0,1},{1,0},{2,3},{3,2},{4,5},{5,4},{6,7},{7,6},{8,9},{9,8},{10,11... | collective-permute-start | bytes 12296 | tf_op jit(solution)/shard_map/ppermute | solution.py:214
  734.4 54.6 %collective-permute-start.4 = (f32[1024,256]{1,0:T(8,128)}, f32[1024,256]{1,0:T(8,128)}, u32[]{:S(2)}, u32[]{:S(2)}) collective-permute-start(f32[1024,256]{1,0:T(8,128)} %fusion.258), channel_id=1, source_target_pairs={{0,1},{1,0},{2,3},{3,2},{4,5},{5,4},{6,7},{7,6},{8,9},{9,8},{10,11... | collective-permute-start | bytes 3145736 | tf_op jit(solution)/shard_map/ppermute | solution.py:214
  779.3 87.7 %collective-permute-start.3 = (f32[1024,1024]{0,1:T(8,128)}, f32[1024,1024]{0,1:T(8,128)}, u32[]{:S(2)}, u32[]{:S(2)}) collective-permute-start(f32[1024,1024]{0,1:T(8,128)} %add_add_fusion.2), channel_id=1, source_target_pairs={{0,1},{1,0},{2,3},{3,2},{4,5},{5,4},{6,7},{7,6},{8,9},{9,8},{10,11... | collective-permute-start | bytes 12582920 | tf_op jit(solution)/shard_map/ppermute | solution.py:214
  795.0 86.4 %copy-start.165 = (f32[768]{0:T(1024)S(1)}, f32[768]{0:T(1024)}, u32[]{:S(2)}) copy-start(f32[768]{0:T(1024)} %get-tuple-element.616) | copy-start | bytes 9220
  795.0 88.0 %copy-start.131 = (f32[1024]{0:T(1024)S(1)}, f32[1024]{0:T(1024)}, u32[]{:S(2)}) copy-start(f32[1024]{0:T(1024)} %get-tuple-element.611) | copy-start | bytes 12292
  899.7 301.0 %reduce-scatter.5.cloned.1.call-start = ((), (), s32[]{:S(2)}) async-start(), calls=%async_computation.3 | async-start | bytes 17825792 | tf_op jit(solution)/shard_map/reduce_scatter | solution.py:229
  973.0 89.7 %copy-start.119 = (f32[1024]{0:T(1024)S(1)}, f32[1024]{0:T(1024)}, u32[]{:S(2)}) copy-start(f32[1024]{0:T(1024)} %copy-done.118) | copy-start | bytes 12292
  973.0 89.7 %copy-start.26 = (f32[1024,1024]{0,1:T(8,128)S(1)}, f32[1024,1024]{0,1:T(8,128)}, u32[]{:S(2)}) copy-start(f32[1024,1024]{0,1:T(8,128)} %get-tuple-element.723) | copy-start | bytes 12582916
  973.0 89.7 %copy-start.27 = (f32[1024,1024]{0,1:T(8,128)S(1)}, f32[1024,1024]{0,1:T(8,128)}, u32[]{:S(2)}) copy-start(f32[1024,1024]{0,1:T(8,128)} %get-tuple-element.719) | copy-start | bytes 12582916
  973.0 86.7 %collective-permute-start.1 = (f32[1024,1024]{0,1:T(8,128)S(1)}, f32[1024,1024]{0,1:T(8,128)S(1)}, u32[]{:S(2)}, u32[]{:S(2)}) collective-permute-start(f32[1024,1024]{0,1:T(8,128)S(1)} %fusion.253), channel_id=1, source_target_pairs={{0,1},{1,0},{2,3},{3,2},{4,5},{5,4},{6,7},{7,6},{8,9},{9,8},{10,11... | collective-permute-start | bytes 12582920 | tf_op jit(solution)/shard_map/ppermute | solution.py:214
  1092.3 115.6 %copy-start.1 = (bf16[1024,1024]{1,0:T(8,128)(2,1)S(1)}, bf16[1024,1024]{1,0:T(8,128)(2,1)}, u32[]{:S(2)}) copy-start(bf16[1024,1024]{1,0:T(8,128)(2,1)} %param.55) | copy-start | bytes 6291460
  (186 other events, 1548.5 us)
Sparse Core Ops, SparseCore 0:
  899.8 119.7 reduce-scatter.2
  1023.7 176.9 reduce-scatter.4

commit v4 on v3

--- a/solution.py
+++ b/solution.py
@@ -392,23 +392,24 @@
             grad_bc_lin, bc_weight.astype(jnp.float32), (((1,), (1,)), ((), ())), precision=PRECISE
         )
     )
-    grad_first, bc_grad_full, conv_bc_grad, conv_bc_bias_grad = tensor_sum(
-        (grad_first_part, bc_part, conv_bc_part, conv_bc_bias_part)
-    )
-    grad_tokens_norm, norm_gain_grad = first_norm_back(grad_first)
+    first_scale = lax.rsqrt(jnp.mean(tokens_wide * tokens_wide, axis=-1, keepdims=True) + EPSILON)
+    norm_gain_part = jnp.sum(grad_first_part * (tokens_wide * first_scale), axis=0)
+    grad_first_part, norm_gain_part = lax.optimization_barrier((grad_first_part, norm_gain_part))
+    grad_first = tensor_sum(grad_first_part)
+    grad_tokens_norm, _ = first_norm_back(grad_first)
     ffn_late, middle_late, _ = lax.optimization_barrier((ffn_full, middle, grad_first))
     block_output = (middle_late + valid_col * ffn_late).astype(jnp.bfloat16)
     tokens_grad = (grad_middle + grad_tokens_norm).astype(jnp.bfloat16)
     early = dp_sum((gate_grad, up_grad), (attn_out_grad, mamba_out_grad, down_grad), ())
     late = dp_sum(
-        (query_grad, key_grad, value_grad, z_grad, x_grad, bc_grad_full, dt_grad),
+        (query_grad, key_grad, value_grad, z_grad, x_grad, bc_part, dt_grad),
         (),
         (
-            norm_gain_grad,
+            norm_gain_part,
             conv_x_grad,
             conv_x_bias_grad,
-            conv_bc_grad,
-            conv_bc_bias_grad,
+            conv_bc_part,
+            conv_bc_bias_part,
             dt_bias_grad,
             a_log_grad,
             skip_grad,
@@ -416,6 +417,8 @@
             ffn_gain_grad,
         ),
     )
+    late = list(late)
+    late[5], late[7], late[10], late[11] = tensor_sum((late[5], late[7], late[10], late[11]))
     matrix_sums = (
         late[0],
         late[1],

time: 1230 us -> 1080 us (0.88)
  waiting for transfers between devices: 430 us -> 333 us
  local copies, waits for them, and re-layouts: 329 us -> 304 us
  matrix products: 250 us -> 235 us
    reduce_scatter x2, waiting for transfers between devices: 107 us -> 7.76 us  [dp_sum(): lax.psum_scatter(jnp.concatenate(pieces, axis=1).reshape(n_dp * lane_rows...]
    unnamed x387 -> x389, local copies, waits for them, and re-layouts: 75.7 us -> 85.7 us
    ppermute x7 -> x8, waiting for transfers between devices: 323 us -> 325 us  [tensor_sum(): swapped = lax.ppermute(values, 'tensor', perm=[(0, 1), (1, 0)])]
  transfers between devices with their start and end apart: 9 -> 10, of which waited for: 5 -> 6; matrix products, arithmetic and copies ran while one was open for 15% -> 13% of each run, Pallas kernels for 0% -> 0%
where the time goes in v4:
time: 1080 us; the launch traced here: 1070 us
  waiting for transfers between devices  333 us (31%)
  local copies, waits for them, and re-layouts  304 us (28%)
  matrix products  235 us (22%)
  other arithmetic  153 us (14%)
  between operations  16.6 us (2%)
  blocking collectives  10.9 us (1%)
    ppermute x8, waiting for transfers between devices, tensor_sum(): swapped = lax.ppermute(values, 'tensor', perm=[(0, 1), (1, 0)])  325 us
    unnamed x389, local copies, waits for them, and re-layouts  85.7 us
    dot_general x3, matrix products, mamba_core(): jnp.einsum('ctsh,cshp->cthp', intersection[..., None] * mixing, scaled, p...  37.7 us
    dynamic_slice x48, local copies, waits for them, and re-layouts, mamba_core(): _, entering = lax.scan(advance, start_state, (pieces, decays, carry_on))  37.2 us
    dot_general x11, matrix products, outer_rows(): lax.dot_general(left, right, (((0,), (0,)), ((), ())), preferred_element_...  34.8 us
    dot_general x11, matrix products, back_project(): lax.dot_general(grad_rows, weight, (((1,), (1,)), ((), ())), preferred_el...  33.1 us
    dot_general x12, matrix products, project(): return jnp.dot(left, right, preferred_element_type=jnp.float32)  32.4 us
    dot_general x3, matrix products, mamba_core(): jnp.einsum('csn,cshp->chnp', write_keys, scaled * to_end[..., None], prec...  27.6 us
  transfers between devices with their start and end apart: 10, of which 6 were waited for; matrix products, arithmetic and copies ran while one was open for 13% of the time, Pallas kernels for 0%

profile of v4, /device:TPU:0, one launch (start us, length us, event | category | flops | bytes accessed | tf_op | source)
XLA Modules:
  0.0 1072.1 jit_solution(9712874697291475829)
XLA Ops:
  66.7 54.7 %while.63 = (s32[]{:T(128)}, f32[12,128,64]{2,1,0:T(8,128)S(1)}, f32[8,12,128,64]{3,2,1,0:T(8,128)}, f32[8,12,1,1]{1,3,2,0:T(1,128)}, f32[8,12]{1,0:T(8,128)S(1)...) while((s32[]{:T(128)}, f32[12,128,64]{2,1,0:T(8,128)S(1)}, ...), condition=%wide.region_11.12_spmd.clone, body=%wide.region_10.11_spmd.clone.sunk | while | flops 589827 | bytes 3933520 | solution.py:120
  121.4 6.2 copy.217
  132.1 13.9 %multiply_reduce_fusion.13 = (f32[8,128]{1,0:T(8,128)S(1)}, f32[8,128,12,64]{1,3,2,0:T(8,128)S(1)}, f32[8,128,12,64]{1,3,2,0:T(8,128)}) fusion(f32[8,128,12,64]{1,0,3,2:T(8,128)S(1)} %bitcast.578, f32[8,128,12,64]{1,0,3,2:T(8,128)S(1)} %bitcast.566, f32[12]{0:T(128)S(1)} %copy-done.174, f32[8,128,12,64]{1,3,2,0:T(8,128)S(1)} %bitcast.580, ...), kind=kOutput, calls=%fused_computation.163 | convolution fusion | flops 1222114304 | bytes 16420912 | tf_op jit(solution)/shard_map/jvp(ctsh,cshp->cthp)/dot_general | solution.py:107
  165.2 25.7 %while.62 = (s32[]{:T(128)}, bf16[2,512,1,4,64]{1,4,3,2,0:T(8,128)(2,1)}, f32[2,1,4,512]{3,2,1,0:T(4,128)}, s32[2]{0:T(128)}, s32[1024]{0:T(1024)S(1)}, /*index=...) while((s32[]{:T(128)}, ...), condition=%wide.region_8.9_spmd.clone, body=%wide.region_5.8_spmd.clone.sunk | while | flops 563608064 | bytes 32717096 | solution.py:159
  214.7 77.1 %collective-permute-done = f32[1024,1024]{0,1:T(8,128)} collective-permute-done((f32[1024,1024]{0,1:T(8,128)}, f32[1024,1024]{0,1:T(8,128)}, u32[]{:S(2)}, u32[]{:S(2)}) %collective-permute-start) | collective-permute-done | bytes 4194336 | tf_op jit(solution)/shard_map/ppermute | solution.py:214
  342.5 72.2 %collective-permute-done.2 = f32[1024,1024]{0,1:T(8,128)} collective-permute-done((f32[1024,1024]{0,1:T(8,128)}, f32[1024,1024]{0,1:T(8,128)}, u32[]{:S(2)}, u32[]{:S(2)}) %collective-permute-start.2) | collective-permute-done | bytes 4194336 | tf_op jit(solution)/shard_map/ppermute | solution.py:214
  420.1 6.3 multiply_convert_fusion
  436.3 7.3 multiply_reduce_fusion.4
  457.0 15.4 %fusion.94 = (f32[8,128,12]{1,2,0:T(8,128)}, f32[8,128,12]{1,2,0:T(8,128)}, f32[8,128,128]{2,1,0:T(8,128)}) fusion(f32[8,128,12]{1,2,0:T(8,128)S(1)} %copy-done.114, f32[8,128,128]{2,1,0:T(8,128)S(1)} %copy-done.90, pred[128,128]{1,0:T(8,128)(4,1)S(1)} %copy-done.144, f32[8,128,12,64]{1,0,3,2:T(8,128)S(1)} %bitcast.567, f32[8,128,12]{1,2,0:T(8,128)S(1)} %copy-done.75, ...), kind=kOutput, calls=%fused_computation.131 | convolution fusion | flops 1222746112 | bytes 7553024 | tf_op jit(solution)/shard_map/transpose(jvp(ctsh,cshp->cthp))/dot_general | solution.py:107
  472.4 11.0 %fusion.157 = f32[8,128,128]{2,1,0:T(8,128)} fusion(f32[8,12,128,64]{3,2,1,0:T(8,128)S(1)} %bitcast.557, f32[8,128,12,64]{1,3,2,0:T(8,128)S(1)} %get-tuple-element.724, f32[8,128,12]{1,2,0:T(8,128)S(1)} %copy-done.81), kind=kOutput, calls=%fused_computation.221 | convolution fusion | flops 1208745984 | bytes 6864896 | tf_op jit(solution)/shard_map/transpose(jvp(ctn,chnp->cthp))/dot_general | solution.py:122
  490.3 44.3 %while.65 = (s32[]{:T(128)}, f32[12,128,64]{2,1,0:T(8,128)S(1)}, f32[8,12,128,64]{3,2,1,0:T(8,128)}, f32[8,12]{1,0:T(8,128)S(1)}, f32[8,12,128,64]{2,3,1,0:T(8,1...) while((s32[]{:T(128)}, f32[12,128,64]{2,1,0:T(8,128)S(1)}, ...), condition=%wide.region_23.24_spmd.clone, body=%wide.region_21.23_spmd.clone.sunk | while | flops 688120 | bytes 4325840 | solution.py:120
  535.2 15.1 %fusion.160 = f32[8,128,128]{2,1,0:T(8,128)} fusion(f32[8,12,128,64]{3,2,1,0:T(8,128)} %get-tuple-element.346, f32[8,128,12,64]{1,0,3,2:T(8,128)} %bitcast.565, f32[8,128,12]{1,2,0:T(8,128)S(1)} %copy-done.78, f32[8,128,12]{1,2,0:T(8,128)S(1)} %copy-done.75), kind=kOutput, calls=%fused_computation.222 | convolution fusion | flops 1209532416 | bytes 6914048 | tf_op jit(solution)/shard_map/transpose(jvp(csn,cshp->chnp))/dot_general | solution.py:111
  550.3 7.1 fusion.73
  559.0 57.9 %while.64 = (s32[]{:T(128)}, f32[1024,1,64]{0,2,1:T(8,128)S(1)}, f32[1024,1,64]{0,2,1:T(8,128)}, f32[2,512,1,4,64]{1,0,4,3,2:T(2,128)}, s32[2]{0:T(128)S(1)}, /*...) while((s32[]{:T(128)}, f32[1024,1,64]{0,2,1:T(8,128)S(1)}, ...), condition=%wide.region_18.19_spmd.clone, body=%wide.region_16.18_spmd.clone.sunk | while | flops 1375664640 | bytes 131012976 | solution.py:205
  646.1 8.4 multiply_reduce_fusion.9
  702.6 8.0 fusion.83
  744.6 11.1 %reshape.828 = f32[20480,128]{1,0:T(8,128)} reshape(f32[16,163840]{1,0:T(8,128)} %dynamic-update-slice.22) | data formatting | bytes 20971520 | tf_op jit(solution)/shard_map/reshape | solution.py:230
  763.1 7.4 copy.264
  770.5 7.1 reshape.837
  806.4 16.0 %reshape.838 = f32[32768,128]{1,0:T(8,128)} reshape(f32[16,262144]{1,0:T(8,128)} %constant_dynamic-update-slice_fusion.12) | data formatting | bytes 33554432 | tf_op jit(solution)/shard_map/reshape | solution.py:230
  830.4 91.4 %collective-permute-done.1 = f32[1024,1024]{0,1:T(8,128)S(1)} collective-permute-done((f32[1024,1024]{0,1:T(8,128)S(1)}, f32[1024,1024]{0,1:T(8,128)S(1)}, u32[]{:S(2)}, u32[]{:S(2)}) %collective-permute-start.1) | collective-permute-done | bytes 4194336 | tf_op jit(solution)/shard_map/ppermute | solution.py:214
  922.8 84.5 %collective-permute-done.3 = f32[1024,1024]{0,1:T(8,128)S(1)} collective-permute-done((f32[1024,1024]{0,1:T(8,128)S(1)}, f32[1024,1024]{0,1:T(8,128)S(1)}, u32[]{:S(2)}, u32[]{:S(2)}) %collective-permute-start.3) | collective-permute-done | bytes 4194336 | tf_op jit(solution)/shard_map/ppermute | solution.py:214
  1016.4 6.2 fusion.89
  1049.8 7.8 reduce-scatter.5.cloned.1.call-done
  (802 shorter events, 567.1 us)
Async XLA Ops:
  7.2 295.3 %copy-start = (bf16[1024,1024]{1,0:T(8,128)(2,1)S(1)}, bf16[1024,1024]{1,0:T(8,128)(2,1)}, u32[]{:S(2)}) copy-start(bf16[1024,1024]{1,0:T(8,128)(2,1)} %param.55) | copy-start | bytes 6291460
  7.2 1019.3 %reduce-scatter.3.cloned.1.call-start = ((), (), s32[]{:S(2)}) async-start(), calls=%async_computation.2 | async-start | bytes 11141120 | tf_op jit(solution)/shard_map/reduce_scatter | solution.py:229
  19.3 36.1 %copy-start.42 = (f32[8,128,12]{2,0,1:T(8,128)}, f32[8,128,12]{2,0,1:T(8,128)S(1)}, u32[]{:S(2)}) copy-start(f32[8,128,12]{2,0,1:T(8,128)S(1)} %fusion.180) | copy-start | bytes 147460
  19.4 112.6 %copy-start.74 = (f32[8,128,12]{1,2,0:T(8,128)}, f32[8,128,12]{1,2,0:T(8,128)S(1)}, u32[]{:S(2)}) copy-start(f32[8,128,12]{1,2,0:T(8,128)S(1)} %copy.210) | copy-start | bytes 147460
  22.3 141.5 %copy-start.109 = (f32[1024]{0:T(1024)}, f32[1024]{0:T(1024)S(1)}, u32[]{:S(2)}) copy-start(f32[1024]{0:T(1024)S(1)} %get-tuple-element.789) | copy-start | bytes 12292
  160.2 32.3 %copy-start.138 = (f32[1024]{0:T(1024)}, f32[1024]{0:T(1024)S(1)}, u32[]{:S(2)}) copy-start(f32[1024]{0:T(1024)S(1)} %get-tuple-element.784) | copy-start | bytes 12292
  200.0 91.8 %collective-permute-start = (f32[1024,1024]{0,1:T(8,128)}, f32[1024,1024]{0,1:T(8,128)}, u32[]{:S(2)}, u32[]{:S(2)}) collective-permute-start(f32[1024,1024]{0,1:T(8,128)} %convolution_add_fusion), channel_id=1, source_target_pairs={{0,1},{1,0},{2,3},{3,2},{4,5},{5,4},{6,7},{7,6},{8,9},{9,8},{10,11... | collective-permute-start | bytes 12582920 | tf_op jit(solution)/shard_map/ppermute | solution.py:214
  212.3 79.5 %copy-start.15 = (bf16[1024,1024]{0,1:T(8,128)(2,1)S(1)}, bf16[1024,1024]{0,1:T(8,128)(2,1)}, u32[]{:S(2)}) copy-start(bf16[1024,1024]{0,1:T(8,128)(2,1)} %copy.207) | copy-start | bytes 6291460
  214.7 82.3 %copy-start.120 = (f32[1024]{0:T(1024)S(1)}, f32[1024]{0:T(1024)}, u32[]{:S(2)}) copy-start(f32[1024]{0:T(1024)} %param.54) | copy-start | bytes 12292
  323.8 90.9 %collective-permute-start.2 = (f32[1024,1024]{0,1:T(8,128)}, f32[1024,1024]{0,1:T(8,128)}, u32[]{:S(2)}, u32[]{:S(2)}) collective-permute-start(f32[1024,1024]{0,1:T(8,128)} %convolution_add_fusion.1), channel_id=1, source_target_pairs={{0,1},{1,0},{2,3},{3,2},{4,5},{5,4},{6,7},{7,6},{8,9},{9,8},{10,11... | collective-permute-start | bytes 12582920 | tf_op jit(solution)/shard_map/ppermute | solution.py:214
  337.9 76.8 %copy-start.12 = (f32[1024,1024]{0,1:T(8,128)S(1)}, f32[1024,1024]{0,1:T(8,128)}, u32[]{:S(2)}) copy-start(f32[1024,1024]{0,1:T(8,128)} %copy-done.11) | copy-start | bytes 12582916
  342.5 77.5 %copy-start.126 = (f32[1024]{0:T(1024)S(1)}, f32[1024]{0:T(1024)}, u32[]{:S(2)}) copy-start(f32[1024]{0:T(1024)} %copy-done.125) | copy-start | bytes 12292
  342.5 77.5 %copy-start.45 = (bf16[1024,1024]{0,1:T(8,128)(2,1)S(1)}, bf16[1024,1024]{0,1:T(8,128)(2,1)}, u32[]{:S(2)}) copy-start(bf16[1024,1024]{0,1:T(8,128)(2,1)} %copy.227) | copy-start | bytes 6291460
  490.3 45.0 %copy-start.78 = (f32[8,128,12]{1,2,0:T(8,128)S(1)}, f32[8,128,12]{1,2,0:T(8,128)}, u32[]{:S(2)}) copy-start(f32[8,128,12]{1,2,0:T(8,128)} %copy-done.77) | copy-start | bytes 147460
  755.7 301.9 %reduce-scatter.5.cloned.1.call-start = ((), (), s32[]{:S(2)}) async-start(), calls=%async_computation.3 | async-start | bytes 17825792 | tf_op jit(solution)/shard_map/reduce_scatter | solution.py:229
  828.3 179.0 %copy-start.17 = (bf16[1024,1024]{0,1:T(8,128)(2,1)S(1)}, bf16[1024,1024]{0,1:T(8,128)(2,1)}, u32[]{:S(2)}) copy-start(bf16[1024,1024]{0,1:T(8,128)(2,1)} %copy.207) | copy-start | bytes 6291460
  828.3 179.0 %copy-start.119 = (f32[1024]{0:T(1024)S(1)}, f32[1024]{0:T(1024)}, u32[]{:S(2)}) copy-start(f32[1024]{0:T(1024)} %param.36) | copy-start | bytes 12292
  828.3 93.5 %collective-permute-start.1 = (f32[1024,1024]{0,1:T(8,128)S(1)}, f32[1024,1024]{0,1:T(8,128)S(1)}, u32[]{:S(2)}, u32[]{:S(2)}) collective-permute-start(f32[1024,1024]{0,1:T(8,128)S(1)} %fusion.255), channel_id=1, source_target_pairs={{0,1},{1,0},{2,3},{3,2},{4,5},{5,4},{6,7},{7,6},{8,9},{9,8},{10,11... | collective-permute-start | bytes 12582920 | tf_op jit(solution)/shard_map/ppermute | solution.py:214
  829.9 177.4 %collective-permute-start.3 = (f32[1024,1024]{0,1:T(8,128)S(1)}, f32[1024,1024]{0,1:T(8,128)S(1)}, u32[]{:S(2)}, u32[]{:S(2)}) collective-permute-start(f32[1024,1024]{0,1:T(8,128)S(1)} %copy-done.27), channel_id=1, source_target_pairs={{0,1},{1,0},{2,3},{3,2},{4,5},{5,4},{6,7},{7,6},{8,9},{9,8},{10,11... | collective-permute-start | bytes 12582920 | tf_op jit(solution)/shard_map/ppermute | solution.py:214
  922.8 87.3 %copy-start.13 = (f32[1024,1024]{0,1:T(8,128)S(1)}, f32[1024,1024]{0,1:T(8,128)}, u32[]{:S(2)}) copy-start(f32[1024,1024]{0,1:T(8,128)} %copy-done.11) | copy-start | bytes 12582916
  1030.0 17.0 %collective-permute-start.4 = (f32[1024]{0:T(1024)S(1)}, f32[1024]{0:T(1024)S(1)}, u32[]{:S(2)}, u32[]{:S(2)}) collective-permute-start(f32[1024]{0:T(1024)S(1)} %get-tuple-element.763), channel_id=1, source_target_pairs={{0,1},{1,0},{2,3},{3,2},{4,5},{5,4},{6,7},{7,6},{8,9},{9,8},{10,11... | collective-permute-start | bytes 12296 | tf_op jit(solution)/shard_map/ppermute | solution.py:214
  1037.4 11.8 %collective-permute-start.5 = (f32[64,256]{1,0:T(8,128)S(1)}, f32[64,256]{1,0:T(8,128)S(1)}, u32[]{:S(2)}, u32[]{:S(2)}) collective-permute-start(f32[64,256]{1,0:T(8,128)S(1)} %reshape.842), channel_id=1, source_target_pairs={{0,1},{1,0},{2,3},{3,2},{4,5},{5,4},{6,7},{7,6},{8,9},{9,8},{10,11... | collective-permute-start | bytes 196616 | tf_op jit(solution)/shard_map/ppermute | solution.py:214
  1038.9 6.8 collective-permute-start.7
  1044.9 3.6 collective-permute-start.6
  (178 other events, 920.0 us)
Sparse Core Ops, SparseCore 0:
  755.8 120.5 reduce-scatter.2
  880.5 176.9 reduce-scatter.4

commit v5 on v4

--- a/solution.py
+++ b/solution.py
@@ -400,9 +400,13 @@
     ffn_late, middle_late, _ = lax.optimization_barrier((ffn_full, middle, grad_first))
     block_output = (middle_late + valid_col * ffn_late).astype(jnp.bfloat16)
     tokens_grad = (grad_middle + grad_tokens_norm).astype(jnp.bfloat16)
-    early = dp_sum((gate_grad, up_grad), (attn_out_grad, mamba_out_grad, down_grad), ())
+    early = dp_sum(
+        (gate_grad, up_grad, query_grad, key_grad, value_grad),
+        (attn_out_grad, mamba_out_grad, down_grad),
+        (),
+    )
     late = dp_sum(
-        (query_grad, key_grad, value_grad, z_grad, x_grad, bc_part, dt_grad),
+        (z_grad, x_grad, bc_part, dt_grad),
         (),
         (
             norm_gain_part,
@@ -418,22 +422,22 @@
         ),
     )
     late = list(late)
-    late[5], late[7], late[10], late[11] = tensor_sum((late[5], late[7], late[10], late[11]))
+    late[2], late[4], late[7], late[8] = tensor_sum((late[2], late[4], late[7], late[8]))
     matrix_sums = (
+        early[2],
+        early[3],
+        early[4],
+        early[5],
         late[0],
         late[1],
         late[2],
-        early[2],
         late[3],
-        late[4],
-        late[5],
-        late[6],
-        early[3],
+        early[6],
         early[0],
         early[1],
-        early[4],
-    )
-    vector_sums = late[7:]
+        early[7],
+    )
+    vector_sums = late[4:]
     return (
         block_output,
         tokens_grad,

time: 1080 us -> 1110 us (1.028)
  matrix products: 235 us -> 248 us
    ppermute x8, waiting for transfers between devices: 325 us -> 305 us  [tensor_sum(): swapped = lax.ppermute(values, 'tensor', perm=[(0, 1), (1, 0)])]
    reduce_scatter x2, waiting for transfers between devices: 7.76 us -> 26.5 us  [dp_sum(): lax.psum_scatter(jnp.concatenate(pieces, axis=1).reshape(n_dp * lane_rows...]
    unnamed x389 -> x368, local copies, waits for them, and re-layouts: 85.7 us -> 82.2 us
where the time goes in v5:
time: 1110 us; the launch traced here: 1090 us
  waiting for transfers between devices  331 us (30%)
  local copies, waits for them, and re-layouts  311 us (28%)
  matrix products  248 us (22%)
  other arithmetic  155 us (14%)
  between operations  16.3 us (1%)
    ppermute x8, waiting for transfers between devices, tensor_sum(): swapped = lax.ppermute(values, 'tensor', perm=[(0, 1), (1, 0)])  305 us
    unnamed x368, local copies, waits for them, and re-layouts  82.2 us
    dot_general x3, matrix products, mamba_core(): jnp.einsum('ctsh,cshp->cthp', intersection[..., None] * mixing, scaled, p...  38.1 us
    dynamic_slice x48, local copies, waits for them, and re-layouts, mamba_core(): _, entering = lax.scan(advance, start_state, (pieces, decays, carry_on))  37.2 us
    dot_general x12, matrix products, project(): return jnp.dot(left, right, preferred_element_type=jnp.float32)  37 us
    dot_general x11, matrix products, outer_rows(): lax.dot_general(left, right, (((0,), (0,)), ((), ())), preferred_element_...  36.3 us
    dot_general x11, matrix products, back_project(): lax.dot_general(grad_rows, weight, (((1,), (1,)), ((), ())), preferred_el...  34.2 us
    reduce_scatter x2, waiting for transfers between devices, dp_sum(): lax.psum_scatter(jnp.concatenate(pieces, axis=1).reshape(n_dp * lane_rows...  26.5 us
  transfers between devices with their start and end apart: 10, of which 6 were waited for; matrix products, arithmetic and copies ran while one was open for 13% of the time, Pallas kernels for 0%

profile of v5, /device:TPU:0, one launch (start us, length us, event | category | flops | bytes accessed | tf_op | source)
XLA Modules:
  0.0 1091.6 jit_solution(2755376520139085934)
XLA Ops:
  25.2 9.9 fusion.138
  58.3 54.7 %while.63 = (s32[]{:T(128)}, f32[12,128,64]{2,1,0:T(8,128)S(1)}, f32[8,12,128,64]{3,2,1,0:T(8,128)}, f32[8,12,1,1]{1,3,2,0:T(1,128)}, f32[8,12]{1,0:T(8,128)S(1)...) while((s32[]{:T(128)}, f32[12,128,64]{2,1,0:T(8,128)S(1)}, ...), condition=%wide.region_11.12_spmd.clone, body=%wide.region_10.11_spmd.clone.sunk | while | flops 589827 | bytes 3934528 | solution.py:120
  113.0 6.6 copy.217
  138.4 13.8 %multiply_reduce_fusion.13 = (f32[8,128]{1,0:T(8,128)S(1)}, f32[8,128,12,64]{1,3,2,0:T(8,128)S(1)}, f32[8,128,12,64]{1,3,2,0:T(8,128)}) fusion(f32[8,128,12,64]{1,0,3,2:T(8,128)S(1)} %bitcast.580, f32[8,128,12,64]{1,0,3,2:T(8,128)S(1)} %bitcast.566, f32[12]{0:T(128)S(1)} %copy-done.162, f32[8,128,12,64]{1,3,2,0:T(8,128)S(1)} %bitcast.579, ...), kind=kOutput, calls=%fused_computation.163 | convolution fusion | flops 1222114304 | bytes 16420912 | tf_op jit(solution)/shard_map/jvp(ctsh,cshp->cthp)/dot_general | solution.py:107
  171.6 26.3 %while.62 = (s32[]{:T(128)}, bf16[2,512,1,4,64]{1,4,3,2,0:T(8,128)(2,1)}, f32[2,1,4,512]{3,2,1,0:T(4,128)}, s32[2]{0:T(128)}, s32[1024]{0:T(1024)S(1)}, /*index=...) while((s32[]{:T(128)}, ...), condition=%wide.region_8.9_spmd.clone, body=%wide.region_5.8_spmd.clone.sunk | while | flops 563608064 | bytes 28392616 | solution.py:159
  221.1 77.9 %collective-permute-done = f32[1024,1024]{0,1:T(8,128)} collective-permute-done((f32[1024,1024]{0,1:T(8,128)}, f32[1024,1024]{0,1:T(8,128)}, u32[]{:S(2)}, u32[]{:S(2)}) %collective-permute-start) | collective-permute-done | bytes 4194336 | tf_op jit(solution)/shard_map/ppermute | solution.py:214
  351.3 7.0 copy.264
  369.0 53.0 %collective-permute-done.2 = f32[1024,1024]{0,1:T(8,128)} collective-permute-done((f32[1024,1024]{0,1:T(8,128)}, f32[1024,1024]{0,1:T(8,128)}, u32[]{:S(2)}, u32[]{:S(2)}) %collective-permute-start.2) | collective-permute-done | bytes 4194336 | tf_op jit(solution)/shard_map/ppermute | solution.py:214
  443.1 7.4 multiply_reduce_fusion.4
  456.8 6.8 multiply_reduce_fusion.10
  463.7 11.0 %fusion.157 = f32[8,128,128]{2,1,0:T(8,128)} fusion(f32[8,12,128,64]{3,2,1,0:T(8,128)S(1)} %bitcast.557, f32[8,128,12,64]{1,3,2,0:T(8,128)S(1)} %get-tuple-element.724, f32[8,128,12]{1,2,0:T(8,128)S(1)} %copy-done.77), kind=kOutput, calls=%fused_computation.221 | convolution fusion | flops 1208745984 | bytes 6864896 | tf_op jit(solution)/shard_map/transpose(jvp(ctn,chnp->cthp))/dot_general | solution.py:122
  474.7 15.3 %fusion.94 = (f32[8,128,12]{1,2,0:T(8,128)}, f32[8,128,12]{1,2,0:T(8,128)}, f32[8,128,128]{2,1,0:T(8,128)}) fusion(f32[8,128,12]{1,2,0:T(8,128)S(1)} %copy-done.106, f32[8,128,128]{2,1,0:T(8,128)S(1)} %copy-done.86, pred[128,128]{1,0:T(8,128)(4,1)S(1)} %copy-done.134, f32[8,128,12,64]{1,0,3,2:T(8,128)S(1)} %bitcast.567, f32[8,128,12]{1,2,0:T(8,128)S(1)} %copy-done.73, ...), kind=kOutput, calls=%fused_computation.131 | convolution fusion | flops 1222746112 | bytes 7553024 | tf_op jit(solution)/shard_map/transpose(jvp(ctsh,cshp->cthp))/dot_general | solution.py:107
  496.8 45.1 %while.65 = (s32[]{:T(128)}, f32[12,128,64]{2,1,0:T(8,128)S(1)}, f32[8,12,128,64]{3,2,1,0:T(8,128)}, f32[8,12]{1,0:T(8,128)S(1)}, f32[8,12,128,64]{2,3,1,0:T(8,1...) while((s32[]{:T(128)}, f32[12,128,64]{2,1,0:T(8,128)S(1)}, ...), condition=%wide.region_23.24_spmd.clone, body=%wide.region_21.23_spmd.clone.sunk | while | flops 688120 | bytes 4325832 | solution.py:120
  541.9 15.1 %fusion.160 = f32[8,128,128]{2,1,0:T(8,128)} fusion(f32[8,12,128,64]{3,2,1,0:T(8,128)} %get-tuple-element.346, f32[8,128,12,64]{1,0,3,2:T(8,128)} %bitcast.565, f32[8,128,12]{1,2,0:T(8,128)S(1)} %copy-done.75, f32[8,128,12]{1,2,0:T(8,128)S(1)} %copy-done.73), kind=kOutput, calls=%fused_computation.222 | convolution fusion | flops 1209532416 | bytes 6914048 | tf_op jit(solution)/shard_map/transpose(jvp(csn,cshp->chnp))/dot_general | solution.py:111
  564.4 9.0 multiply_reduce_fusion.9
  581.6 6.3 multiply_reduce_fusion.8
  625.2 71.0 %while.64 = (s32[]{:T(128)}, f32[1024,1,64]{0,2,1:T(8,128)S(1)}, f32[1024,1,64]{0,2,1:T(8,128)}, f32[2,512,1,4,64]{1,0,4,3,2:T(2,128)}, s32[2]{0:T(128)}, /*inde...) while((s32[]{:T(128)}, f32[1024,1,64]{0,2,1:T(8,128)S(1)}, ...), condition=%wide.region_18.19_spmd.clone, body=%wide.region_16.18_spmd.clone.sunk | while | flops 1375664640 | bytes 127343016 | solution.py:205
  641.4 10.4 dynamic_update_slice.61
  676.6 10.4 dynamic_update_slice.61
  734.4 11.6 %fusion.83 = (f32[1024]{0:T(1024)S(1)}, f32[1024,1024]{0,1:T(8,128)}) fusion(bf16[1024,1024]{0,1:T(8,128)(2,1)S(1)} %copy-done.13, f32[1024]{0:T(1024)S(1)} %copy-done.100, f32[1024,256]{1,0:T(8,128)S(1)} %get-tuple-element.760, bf16[1024,256]{1,0:T(8,128)(2,1)} %param.43, f32[1024,1024]{0,1:T(8,128)} %fusion.216, f32[1024,1024]{0,1:T(8,128)} %fusion.257, ...), kind=kOutput, calls=%fused_computation.110 | convolution fusion | flops 3231710208 | bytes 33038336 | tf_op jit(solution)/shard_map/dot_general | solution.py:391
  811.5 17.5 %reshape.835 = f32[36864,128]{1,0:T(8,128)} reshape(f32[16,294912]{1,0:T(8,128)} %broadcast_dynamic-update-slice_fusion) | data formatting | bytes 37748736 | tf_op jit(solution)/shard_map/reshape | solution.py:230
  836.0 91.4 %collective-permute-done.1 = f32[1024,1024]{0,1:T(8,128)S(1)} collective-permute-done((f32[1024,1024]{0,1:T(8,128)S(1)}, f32[1024,1024]{0,1:T(8,128)S(1)}, u32[]{:S(2)}, u32[]{:S(2)}) %collective-permute-start.1) | collective-permute-done | bytes 4194336 | tf_op jit(solution)/shard_map/ppermute | solution.py:214
  930.4 82.2 %collective-permute-done.3 = f32[1024,1024]{0,1:T(8,128)S(1)} collective-permute-done((f32[1024,1024]{0,1:T(8,128)S(1)}, f32[1024,1024]{0,1:T(8,128)S(1)}, u32[]{:S(2)}, u32[]{:S(2)}) %collective-permute-start.3) | collective-permute-done | bytes 4194336 | tf_op jit(solution)/shard_map/ppermute | solution.py:214
  1047.3 26.5 %reduce-scatter.5.cloned.1.call-done = f32[2304,128]{1,0:T(8,128)} async-done(((f32[36864,128]{1,0:T(8,128)}), f32[2304,128]{1,0:T(8,128)}) %reduce-scatter.5.cloned.1.call-update) | async-done | bytes 1179664 | tf_op jit(solution)/shard_map/reduce_scatter | solution.py:229
  (774 shorter events, 576.8 us)
Async XLA Ops:
  7.2 302.6 %copy-start = (bf16[1024,1024]{1,0:T(8,128)(2,1)S(1)}, bf16[1024,1024]{1,0:T(8,128)(2,1)}, u32[]{:S(2)}) copy-start(bf16[1024,1024]{1,0:T(8,128)(2,1)} %param.55) | copy-start | bytes 6291460
  7.2 1019.8 %reduce-scatter.3.cloned.1.call-start = ((), (), s32[]{:S(2)}) async-start(), calls=%async_computation.2 | async-start | bytes 8912896 | tf_op jit(solution)/shard_map/reduce_scatter | solution.py:229
  17.4 120.1 %copy-start.72 = (f32[8,128,12]{1,2,0:T(8,128)}, f32[8,128,12]{1,2,0:T(8,128)S(1)}, u32[]{:S(2)}) copy-start(f32[8,128,12]{1,2,0:T(8,128)S(1)} %copy.210) | copy-start | bytes 147460
  18.5 119.0 %copy-start.133 = (pred[128,128]{1,0:T(8,128)(4,1)}, pred[128,128]{1,0:T(8,128)(4,1)S(1)}, u32[]{:S(2)}) copy-start(pred[128,128]{1,0:T(8,128)(4,1)S(1)} %iota_compare_fusion.2) | copy-start | bytes 49156
  18.5 151.7 %copy-start.146 = (f32[32]{0:T(128)}, f32[32]{0:T(128)S(1)}, u32[]{:S(2)}) copy-start(f32[32]{0:T(128)S(1)} %multiply_power_fusion) | copy-start | bytes 388
  25.0 145.2 %copy-start.101 = (f32[1024]{0:T(1024)}, f32[1024]{0:T(1024)S(1)}, u32[]{:S(2)}) copy-start(f32[1024]{0:T(1024)S(1)} %get-tuple-element.789) | copy-start | bytes 12292
  25.1 402.2 %copy-start.103 = (f32[1024]{0:T(1024)}, f32[1024]{0:T(1024)S(1)}, u32[]{:S(2)}) copy-start(f32[1024]{0:T(1024)S(1)} %get-tuple-element.785) | copy-start | bytes 12292
  207.3 91.8 %collective-permute-start = (f32[1024,1024]{0,1:T(8,128)}, f32[1024,1024]{0,1:T(8,128)}, u32[]{:S(2)}, u32[]{:S(2)}) collective-permute-start(f32[1024,1024]{0,1:T(8,128)} %convolution_add_fusion), channel_id=1, source_target_pairs={{0,1},{1,0},{2,3},{3,2},{4,5},{5,4},{6,7},{7,6},{8,9},{9,8},{10,11... | collective-permute-start | bytes 12582920 | tf_op jit(solution)/shard_map/ppermute | solution.py:214
  218.7 80.4 %copy-start.12 = (bf16[1024,1024]{0,1:T(8,128)(2,1)S(1)}, bf16[1024,1024]{0,1:T(8,128)(2,1)}, u32[]{:S(2)}) copy-start(bf16[1024,1024]{0,1:T(8,128)(2,1)} %copy.207) | copy-start | bytes 6291460
  221.1 83.1 %copy-start.114 = (f32[1024]{0:T(1024)S(1)}, f32[1024]{0:T(1024)}, u32[]{:S(2)}) copy-start(f32[1024]{0:T(1024)} %param.54) | copy-start | bytes 12292
  331.1 90.9 %collective-permute-start.2 = (f32[1024,1024]{0,1:T(8,128)}, f32[1024,1024]{0,1:T(8,128)}, u32[]{:S(2)}, u32[]{:S(2)}) collective-permute-start(f32[1024,1024]{0,1:T(8,128)} %convolution_add_fusion.1), channel_id=1, source_target_pairs={{0,1},{1,0},{2,3},{3,2},{4,5},{5,4},{6,7},{7,6},{8,9},{9,8},{10,11... | collective-permute-start | bytes 12582920 | tf_op jit(solution)/shard_map/ppermute | solution.py:214
  364.4 57.6 %copy-start.10 = (f32[1024,1024]{0,1:T(8,128)S(1)}, f32[1024,1024]{0,1:T(8,128)}, u32[]{:S(2)}) copy-start(f32[1024,1024]{0,1:T(8,128)} %copy-done.9) | copy-start | bytes 12582916
  369.0 58.3 %copy-start.40 = (bf16[1024,1024]{0,1:T(8,128)(2,1)S(1)}, bf16[1024,1024]{0,1:T(8,128)(2,1)}, u32[]{:S(2)}) copy-start(bf16[1024,1024]{0,1:T(8,128)(2,1)} %copy.227) | copy-start | bytes 6291460
  496.8 45.1 %copy-start.75 = (f32[8,128,12]{1,2,0:T(8,128)S(1)}, f32[8,128,12]{1,2,0:T(8,128)}, u32[]{:S(2)}) copy-start(f32[8,128,12]{1,2,0:T(8,128)} %copy-done.74) | copy-start | bytes 147460
  771.1 302.6 %reduce-scatter.5.cloned.1.call-start = ((), (), s32[]{:S(2)}) async-start(), calls=%async_computation.3 | async-start | bytes 20054016 | tf_op jit(solution)/shard_map/reduce_scatter | solution.py:229
  833.9 178.7 %copy-start.113 = (f32[1024]{0:T(1024)S(1)}, f32[1024]{0:T(1024)}, u32[]{:S(2)}) copy-start(f32[1024]{0:T(1024)} %param.36) | copy-start | bytes 12292
  833.9 93.5 %collective-permute-start.1 = (f32[1024,1024]{0,1:T(8,128)S(1)}, f32[1024,1024]{0,1:T(8,128)S(1)}, u32[]{:S(2)}, u32[]{:S(2)}) collective-permute-start(f32[1024,1024]{0,1:T(8,128)S(1)} %fusion.255), channel_id=1, source_target_pairs={{0,1},{1,0},{2,3},{3,2},{4,5},{5,4},{6,7},{7,6},{8,9},{9,8},{10,11... | collective-permute-start | bytes 12582920 | tf_op jit(solution)/shard_map/ppermute | solution.py:214
  835.4 177.2 %collective-permute-start.3 = (f32[1024,1024]{0,1:T(8,128)S(1)}, f32[1024,1024]{0,1:T(8,128)S(1)}, u32[]{:S(2)}, u32[]{:S(2)}) collective-permute-start(f32[1024,1024]{0,1:T(8,128)S(1)} %copy-done.23), channel_id=1, source_target_pairs={{0,1},{1,0},{2,3},{3,2},{4,5},{5,4},{6,7},{7,6},{8,9},{9,8},{10,11... | collective-permute-start | bytes 12582920 | tf_op jit(solution)/shard_map/ppermute | solution.py:214
  930.4 83.0 %copy-start.118 = (f32[1024]{0:T(1024)S(1)}, f32[1024]{0:T(1024)}, u32[]{:S(2)}) copy-start(f32[1024]{0:T(1024)} %copy-done.117) | copy-start | bytes 12292
  930.4 83.0 %copy-start.25 = (f32[1024,1024]{0,1:T(8,128)S(1)}, f32[1024,1024]{0,1:T(8,128)}, u32[]{:S(2)}) copy-start(f32[1024,1024]{0,1:T(8,128)} %get-tuple-element.726) | copy-start | bytes 12582916
  1030.4 13.0 %collective-permute-start.7 = (f32[256]{0:T(256)S(1)}, f32[256]{0:T(256)S(1)}, u32[]{:S(2)}, u32[]{:S(2)}) collective-permute-start(f32[256]{0:T(256)S(1)} %slice_bitcast_fusion.4), channel_id=1, source_target_pairs={{0,1},{1,0},{2,3},{3,2},{4,5},{5,4},{6,7},{7,6},{8,9},{9,8},{10,11... | collective-permute-start | bytes 3080 | tf_op jit(solution)/shard_map/ppermute | solution.py:214
  1032.2 13.8 %collective-permute-start.6 = (f32[4,256]{1,0:T(4,128)S(1)}, f32[4,256]{1,0:T(4,128)S(1)}, u32[]{:S(2)}, u32[]{:S(2)}) collective-permute-start(f32[4,256]{1,0:T(4,128)S(1)} %reshape.845), channel_id=1, source_target_pairs={{0,1},{1,0},{2,3},{3,2},{4,5},{5,4},{6,7},{7,6},{8,9},{9,8},{10,11... | collective-permute-start | bytes 12296 | tf_op jit(solution)/shard_map/ppermute | solution.py:214
  1034.1 12.6 %collective-permute-start.5 = (f32[64,256]{1,0:T(8,128)S(1)}, f32[64,256]{1,0:T(8,128)S(1)}, u32[]{:S(2)}, u32[]{:S(2)}) collective-permute-start(f32[64,256]{1,0:T(8,128)S(1)} %reshape.842), channel_id=1, source_target_pairs={{0,1},{1,0},{2,3},{3,2},{4,5},{5,4},{6,7},{7,6},{8,9},{9,8},{10,11... | collective-permute-start | bytes 196616 | tf_op jit(solution)/shard_map/ppermute | solution.py:214
  1041.1 3.6 collective-permute-start.4
  (164 other events, 972.4 us)
Sparse Core Ops, SparseCore 0:
  771.3 104.6 reduce-scatter.2
  880.0 193.6 reduce-scatter.4
